TPU v7x, 32 devices: a whole 2x2x4 slice. The times are simulated.
32 devices in a mesh: dp: 4 (over y, x), expert: 8 (over z, core).
Axes of the slice: x: 2, y: 2, z: 4, core: 2. Of those that a mesh axis runs over, the one named last changes fastest.
Arguments:
- context: bfloat16 [8, 4, 128, 1536], P('expert', None, None, 'dp'), may hold values from -0.29882812 to 0.29882812
- w_proj: bfloat16 [1536, 1536], P('dp'), may hold values from -0.15625 to 0.15625
- residual: bfloat16 [4096, 1536], P(('dp', 'expert')), may hold values from -0.29882812 to 0.29882812
- gain_first: float32 [1536], replicated, may hold values from 0.25 to 1.75
- gain_next: float32 [1536], replicated, may hold values from 0.25 to 1.75
- w_router: bfloat16 [1536, 40], replicated, may hold values from -0.15625 to 0.15625
- expert_ids: int32 [4096, 8], P(('dp', 'expert')), may hold values from 0 to 39, all different within a row
- replica_pick: int32 [4096, 8], P(('dp', 'expert')), may hold values from 0 to 5039
- slot_expert: int32 [48], replicated, may hold values from 0 to 39, as said below
- cap_blocks: int32 [48], replicated, may hold values from 1 to 4
- w_in: bfloat16 [48, 1536, 1024], P('expert', 'dp'), as said below
- w_out: bfloat16 [48, 512, 1536], P('expert', 'dp'), as said below
Outputs:
- residual_out: bfloat16 [4096, 1536], P(('dp', 'expert'))
- next_normed: bfloat16 [4096, 1536], P(('dp', 'expert'))
Inputs may be any that keep to these rules, and one draw needn't show every extreme that they name: `slot_expert`: every expert is held by at least one slot; slot s lies on index s // 6 of the expert axis. `w_in`: two slots that hold the same expert have equal weights. `w_out`: two slots that hold the same expert have equal weights.
All inputs are finite; a program needn't handle non-finite values.
Results may differ from a plain program's by a relative error of at most 0.01.
Values may be sent and summed in bfloat16 or wider, within the bound.
No kernel may reach another device: no remote copies, remote signals or barrier semaphores. Data moves between devices by JAX's collectives and lax.ppermute only.
A program may use at most 128 MiB of HBM per device.

v0:
```python
import math

import jax
import jax.numpy as jnp
from jax import lax
from jax.sharding import PartitionSpec as P


CAP_UNIT = 8
CAP_MOST = 32


def rms_scale(values, gain):
    widened = values.astype(jnp.float32)
    return widened * lax.rsqrt(jnp.mean(widened * widened, axis=-1, keepdims=True) + 1e-06) * gain


def route_rows(normed, w_router, expert_ids, replica_pick, slot_expert, cap_blocks, cap_unit):
    blocks, row_count, topk_all = expert_ids.shape
    experts_all = w_router.shape[1]
    slots_all = slot_expert.shape[0]
    logits = jnp.dot(normed, w_router, preferred_element_type=jnp.float32)
    logits = logits.reshape(blocks, row_count, experts_all)
    expert_axis = jnp.arange(experts_all)
    one_hot = expert_ids[..., None] == expert_axis
    chosen = jnp.sum(jnp.where(one_hot, logits[:, :, None, :], jnp.float32(0.0)), axis=-1)
    raised = jnp.exp(chosen)
    gates = raised / jnp.sum(raised, axis=-1, keepdims=True)
    holder = (slot_expert[None, :] == expert_axis[:, None]).astype(jnp.int32)
    rep_count = jnp.sum(holder, axis=1)
    earlier = jnp.cumsum(holder, axis=1) - holder
    slot_rank = jnp.sum(earlier * holder, axis=0)
    count_of = jnp.sum(jnp.where(one_hot, rep_count, 0), axis=-1)
    replica = replica_pick % count_of
    slot_axis = jnp.arange(slots_all)
    matched = (slot_expert == expert_ids[..., None]) & (slot_rank == replica[..., None])
    target_slot = jnp.sum(jnp.where(matched, slot_axis, 0), axis=-1)
    flat_count = row_count * topk_all
    selected = matched.reshape(blocks, flat_count, slots_all)
    flat_axis = lax.optimization_barrier(jnp.arange(flat_count))
    lower = (flat_axis[:, None] > flat_axis[None, :]).astype(jnp.bfloat16)
    before = jnp.einsum(
        "ij,bjs->bis", lower, selected.astype(jnp.bfloat16), preferred_element_type=jnp.float32
    )
    position = (
        jnp.sum(jnp.where(selected, before, jnp.float32(0.0)), axis=-1)
        .astype(jnp.int32)
        .reshape(blocks, row_count, topk_all)
    )
    capacity = (
        jnp.sum(jnp.where(target_slot[..., None] == slot_axis, cap_blocks, 0), axis=-1) * cap_unit
    )
    retained = position < capacity
    return (gates, target_slot, position, retained)


def unit_plan(slot_local, n_dp, hidden_units):
    full = slot_local // n_dp
    rest = slot_local - full * n_dp
    chunks = n_dp // math.gcd(rest, n_dp) if rest else 1
    halves = rest * chunks // n_dp
    chunk_width = hidden_units // chunks
    owned_full = [[o * full + j for j in range(full)] for o in range(n_dp)]
    if halves == 1 and rest * chunks == n_dp:
        owned_part = [[(full * n_dp + o % rest, o // rest)] for o in range(n_dp)]
    else:
        owned_part = [
            [(full * n_dp + (o * halves + i) // chunks, (o * halves + i) % chunks)
             for i in range(halves)]
            for o in range(n_dp)
        ]
    return full, halves, chunks, chunk_width, owned_full, owned_part


def on_device_body(
    context,
    w_proj,
    residual,
    gain_first,
    gain_next,
    w_router,
    expert_ids,
    replica_pick,
    slot_expert,
    cap_blocks,
    w_in,
    w_out,
):
    tok_rows, model_width = residual.shape
    topk_all = expert_ids.shape[1]
    slot_local, d_local, _ = w_in.shape
    hidden_units = w_in.shape[2] // 2
    ff_local = w_out.shape[1]
    n_dp = lax.axis_size("dp")
    n_exp = lax.axis_size("expert")
    dp_at = lax.axis_index("dp")
    exp_at = lax.axis_index("expert")
    full, halves, chunks, chunk_width, owned_full, owned_part = unit_plan(
        slot_local, n_dp, hidden_units
    )
    sources_per_chunk = chunk_width // ff_local
    rest = slot_local - full * n_dp
    paired = (
        halves == 1 and rest * chunks == n_dp and chunk_width == rest * ff_local
    )
    lane_width = 2 * chunk_width if (ff_local * model_width) % (2 * chunk_width) == 0 else 128

    def as_rows(piece):
        return piece.reshape(-1, lane_width)

    weight_parts = []
    for o in range(n_dp):
        pieces = []
        for s in owned_full[o]:
            pieces += [as_rows(w_in[s]), as_rows(w_out[s])]
        for s, c in owned_part[o]:
            lo = c * chunk_width
            pieces += [
                as_rows(w_in[s, :, lo:lo + chunk_width]),
                as_rows(w_in[s, :, hidden_units + lo:hidden_units + lo + chunk_width]),
            ]
            if not paired:
                pieces.append(as_rows(w_out[s]))
        weight_parts.append(jnp.concatenate(pieces, axis=0))
    weight_recv = lax.all_to_all(jnp.stack(weight_parts), "dp", 0, 0, tiled=True)
    offset = 0

    def take(shape):
        nonlocal offset
        count = math.prod(shape) // lane_width
        piece = weight_recv[:, offset:offset + count].reshape((n_dp,) + shape)
        offset += count
        return piece

    full_in, full_out, part_in, part_out = [], [], [], []
    for _ in range(full):
        full_in.append(take((d_local, 2 * hidden_units)).reshape(n_dp * d_local, 2 * hidden_units))
        full_out.append(take((ff_local, model_width)).reshape(n_dp * ff_local, model_width))
    for _ in range(halves):
        gate_in = take((d_local, chunk_width))
        up_in = take((d_local, chunk_width))
        part_in.append(
            jnp.concatenate([gate_in, up_in], axis=-1).reshape(n_dp * d_local, 2 * chunk_width)
        )
        if not paired:
            part_out.append(take((ff_local, model_width)))
    if paired:
        group_at = dp_at % rest
        held = [lax.dynamic_index_in_dim(w_out, full * n_dp + group_at, 0, keepdims=False)]
        for k in range(1, rest):
            sent = lax.dynamic_index_in_dim(
                w_out, full * n_dp + (group_at + rest - k) % rest, 0, keepdims=False
            )
            pairs = [
                (base + (p + k) % rest, base + p)
                for base in range(0, n_dp, rest)
                for p in range(rest)
            ]
            held.append(lax.ppermute(sent, "dp", pairs))
        part_out.append(
            jnp.roll(jnp.stack(held), group_at, axis=0).reshape(chunk_width, model_width)
        )

    ids_all = lax.all_gather(
        jnp.concatenate([expert_ids, replica_pick], axis=1), "expert", axis=0, tiled=True
    ).reshape(n_exp, tok_rows, 2 * topk_all)

    flat_context = context.reshape(-1, context.shape[3])
    attended = lax.psum_scatter(
        jnp.dot(flat_context, w_proj, preferred_element_type=jnp.float32),
        "dp",
        scatter_dimension=0,
        tiled=True,
    )
    hidden_state = (residual.astype(jnp.float32) + attended.astype(jnp.float32)).astype(
        jnp.bfloat16
    )
    normed = rms_scale(hidden_state, gain_first).astype(jnp.bfloat16)

    normed_all = lax.all_gather(normed, "expert", axis=0, tiled=True)
    gates, target_slot, position, retained = route_rows(
        normed_all,
        w_router,
        ids_all[:, :, :topk_all],
        ids_all[:, :, topk_all:],
        slot_expert,
        cap_blocks,
        CAP_UNIT,
    )
    here = retained & (target_slot // slot_local == exp_at)
    local = jnp.where(here, (target_slot % slot_local) * CAP_MOST + position, -1)
    hit = local[..., None] == jnp.arange(slot_local * CAP_MOST)
    pick = jnp.any(hit, axis=2).astype(jnp.bfloat16)
    weight = jnp.sum(jnp.where(hit, gates[..., None], jnp.float32(0.0)), axis=2)
    slot_in = jnp.einsum(
        "btr,btd->brd",
        pick,
        normed_all.reshape(n_exp, tok_rows, model_width),
        preferred_element_type=jnp.float32,
    ).astype(jnp.bfloat16)
    slot_in = slot_in.reshape(n_exp, slot_local, CAP_MOST, model_width)

    x_parts = []
    for o in range(n_dp):
        x_parts.append(
            jnp.stack([slot_in[:, s] for s in owned_full[o]] + [slot_in[:, s] for s, _ in owned_part[o]])
        )
    x_recv = lax.all_to_all(jnp.stack(x_parts), "dp", 0, 0, tiled=True)

    unit_rows = n_dp * n_exp * CAP_MOST

    def expert_rows(rows, w_up, w_down, width):
        gate_up = jnp.dot(rows, w_up, preferred_element_type=jnp.float32)
        activated = (jax.nn.silu(gate_up[:, :width]) * gate_up[:, width:]).astype(jnp.bfloat16)
        return jnp.dot(activated, w_down, preferred_element_type=jnp.float32).astype(jnp.bfloat16)

    outs = []
    for j in range(full):
        rows = x_recv[:, j].reshape(unit_rows, model_width)
        outs.append(expert_rows(rows, full_in[j], full_out[j], hidden_units))
    for i in range(halves):
        rows = x_recv[:, full + i].reshape(unit_rows, model_width)
        if paired:
            w_down = part_out[i]
        else:
            chunk_at = (dp_at * halves + i) % chunks
            w_down = lax.dynamic_slice_in_dim(
                part_out[i], chunk_at * sources_per_chunk, sources_per_chunk, axis=0
            ).reshape(chunk_width, model_width)
        outs.append(expert_rows(rows, part_in[i], w_down, chunk_width))
    y_send = (
        jnp.stack(outs)
        .reshape(full + halves, n_dp, n_exp, CAP_MOST, model_width)
        .transpose(1, 0, 2, 3, 4)
    )
    weight_hi = weight.astype(jnp.bfloat16)
    weight_lo = (weight - weight_hi.astype(jnp.float32)).astype(jnp.bfloat16)
    halves_d = 2 if model_width % 256 == 0 else 1
    piece_width = model_width // halves_d
    combined_parts = []
    for h in range(halves_d):
        cols = slice(h * piece_width, (h + 1) * piece_width)
        y_recv = lax.all_to_all(y_send[..., cols], "dp", 0, 0, tiled=True)
        slot_out = [None] * slot_local
        for o in range(n_dp):
            for j, s in enumerate(owned_full[o]):
                slot_out[s] = y_recv[o, j]
            for i, (s, _) in enumerate(owned_part[o]):
                part = y_recv[o, full + i].astype(jnp.float32)
                slot_out[s] = part if slot_out[s] is None else slot_out[s] + part
        slot_out = [part.astype(jnp.bfloat16) for part in slot_out]
        expert_out = jnp.stack(slot_out, axis=1).reshape(
            n_exp, slot_local * CAP_MOST, piece_width
        )
        partial = jnp.einsum(
            "btr,brd->btd", weight_hi, expert_out, preferred_element_type=jnp.float32
        ) + jnp.einsum("btr,brd->btd", weight_lo, expert_out, preferred_element_type=jnp.float32)
        combined_parts.append(
            lax.psum_scatter(
                partial.reshape(n_exp * tok_rows, piece_width).astype(jnp.bfloat16),
                "expert",
                scatter_dimension=0,
                tiled=True,
            )
        )
    combined = jnp.concatenate(combined_parts, axis=-1)
    residual_out = (hidden_state.astype(jnp.float32) + combined.astype(jnp.float32)).astype(
        jnp.bfloat16
    )
    next_normed = rms_scale(residual_out, gain_next).astype(jnp.bfloat16)
    return (residual_out, next_normed)


def solution(mesh):
    placed = (
        P("expert", None, None, "dp"),
        P("dp", None),
        P(("dp", "expert"), None),
        P(),
        P(),
        P(),
        P(("dp", "expert"), None),
        P(("dp", "expert"), None),
        P(),
        P(),
        P("expert", "dp", None),
        P("expert", "dp", None),
    )
    return jax.shard_map(
        on_device_body,
        mesh=mesh,
        in_specs=placed,
        out_specs=(P(("dp", "expert"), None), P(("dp", "expert"), None)),
        check_vma=False,
    )
```

profile of v0, /device:TPU:0, one launch (start us, length us, event | category | flops | bytes accessed | tf_op | source)
XLA Modules:
  0.0 413.3 jit_solution(11537969740410243941)
XLA Ops:
  8.4 3.6 fusion.76
  12.1 46.7 %reduce-scatter.4.cloned.1.call-done = f32[128,1536]{1,0:T(8,128)} async-done(((f32[512,1536]{1,0:T(8,128)}), f32[128,1536]{1,0:T(8,128)}) %reduce-scatter.4.cloned.1.call-update) | async-done | bytes 786448 | tf_op jit(solution)/shard_map/reduce_scatter | solution.py:169
  68.7 2.8 fusion.74
  74.5 3.5 fusion.72
  82.2 4.6 %maximum_bitcast_fusion.3 = (bf16[1,1536,512]{2,1,0:T(8,128)(2,1)S(1)}, bf16[1,1536,512]{2,1,0:T(8,128)(2,1)S(1)}) fusion(bf16[192,512]{1,0:T(8,128)(2,1)} %reshape_squeeze.66, bf16[192,512]{1,0:T(8,128)(2,1)} %reshape_squeeze.65, bf16[384,512]{1,0:T(8,128)(2,1)} %reshape_squeeze.64, bf16[768,512]{1,0:T(8,128)(2,1)} %reshape_squeeze.63, ...), kind=kLoop, calls=%fused_computation.28 | loop fusion | flops 12582912 | bytes 6291456 | tf_op jit(solution)/shard_map/stack | solution.py:125
  87.1 3.1 pad_maximum_fusion.1
  90.2 5.4 %all-to-all-start.1 = ((bf16[4,1536,512]{2,1,0:T(8,128)(2,1)}), bf16[4,1536,512]{2,1,0:T(8,128)(2,1)}, u32[]{:S(2)}, u32[]{:S(2)}) async-start(bf16[4,1536,512]{2,1,0:T(8,128)(2,1)} %pad_maximum_fusion.1), calls=%async_computation.2 | async-start | bytes 12582912 | tf_op jit(solution)/shard_map/all_to_all | solution.py:125
  95.6 14.2 %all_gather.6 = s32[1024,16]{0,1:T(8,128)S(1)} all-gather(s32[128,16]{0,1:T(8,128)S(1)} %pad_add_fusion), channel_id=1, replica_groups=mesh['dp'=4,'expert'=8] {'expert'}, dimensions={0}, use_global_device_ids=true | all-gather | bytes 73728 | tf_op jit(solution)/shard_map/all_gather | solution.py:164
  116.5 3.3 convolution_convert_fusion
  120.9 3.4 pad_maximum_fusion
  124.2 41.2 %all-to-all-done.1 = bf16[4,1536,512]{2,1,0:T(8,128)(2,1)} async-done(((bf16[4,1536,512]{2,1,0:T(8,128)(2,1)}), bf16[4,1536,512]{2,1,0:T(8,128)(2,1)}, u32[]{:S(2)}, u32[]{:S(2)}) %all-to-all-start.1) | async-done | bytes 6291488 | tf_op jit(solution)/shard_map/all_to_all | solution.py:125
  165.4 5.5 %all-to-all-start = ((bf16[4,2,8,32,1536]{4,3,2,1,0:T(8,128)(2,1)}), bf16[4,2,8,32,1536]{4,3,2,1,0:T(8,128)(2,1)}, u32[]{:S(2)}, u32[]{:S(2)}) async-start(bf16[4,2,8,32,1536]{4,3,2,1,0:T(8,128)(2,1)} %pad_maximum_fusion), calls=%async_computation.1 | async-start | bytes 12582912 | tf_op jit(solution)/shard_map/all_to_all | solution.py:208
  172.7 75.7 %collective-permute-done = bf16[128,1536]{1,0:T(8,128)(2,1)S(1)} collective-permute-done((bf16[128,1536]{1,0:T(8,128)(2,1)S(1)}, bf16[128,1536]{1,0:T(8,128)(2,1)S(1)}, u32[]{:S(2)}, u32[]{:S(2)}) %collective-permute-start) | collective-permute-done | bytes 393248 | tf_op jit(solution)/shard_map/ppermute | solution.py:159
  253.0 3.8 slice.219
  256.9 5.7 %reshape_reshape.6 = bf16[1536,1024]{1,0:T(8,128)(2,1)} reshape(bf16[4,768,512]{2,1,0:T(8,128)(2,1)} %slice.219) | data formatting | bytes 6291456 | tf_op jit(solution)/shard_map/reshape;reshape | solution.py:137
  264.6 3.4 fusion.70
  268.4 3.4 fusion.77
  277.0 3.5 fusion.69
  280.5 4.8 %all-to-all-start.2 = ((bf16[4,2,8,32,768]{4,3,2,1,0:T(8,128)(2,1)}), bf16[4,2,8,32,768]{4,3,2,1,0:T(8,128)(2,1)}, u32[]{:S(2)}, u32[]{:S(2)}) async-start(bf16[4,2,8,32,768]{4,3,2,1,0:T(8,128)(2,1)} %get-tuple-element.8), calls=%async_computation.3 | async-start | bytes 6291456 | tf_op jit(solution)/shard_map/all_to_all | solution.py:243
  285.3 2.9 convolution_bitcast_fusion
  289.7 30.5 %all-to-all-done.2 = bf16[4,2,8,32,768]{4,3,2,1,0:T(8,128)(2,1)} async-done(((bf16[4,2,8,32,768]{4,3,2,1,0:T(8,128)(2,1)}), bf16[4,2,8,32,768]{4,3,2,1,0:T(8,128)(2,1)}, u32[]{:S(2)}, u32[]{:S(2)}) %all-to-all-start.2) | async-done | bytes 3145760 | tf_op jit(solution)/shard_map/all_to_all | solution.py:243
  320.2 4.6 %all-to-all-start.3 = ((bf16[4,2,8,32,768]{4,3,2,1,0:T(8,128)(2,1)}), bf16[4,2,8,32,768]{4,3,2,1,0:T(8,128)(2,1)}, u32[]{:S(2)}, u32[]{:S(2)}) async-start(bf16[4,2,8,32,768]{4,3,2,1,0:T(8,128)(2,1)} %get-tuple-element.9), calls=%async_computation.5 | async-start | bytes 6291456 | tf_op jit(solution)/shard_map/all_to_all | solution.py:243
  334.4 26.1 %all-to-all-done.3 = bf16[4,2,8,32,768]{4,3,2,1,0:T(8,128)(2,1)} async-done(((bf16[4,2,8,32,768]{4,3,2,1,0:T(8,128)(2,1)}), bf16[4,2,8,32,768]{4,3,2,1,0:T(8,128)(2,1)}, u32[]{:S(2)}, u32[]{:S(2)}) %all-to-all-start.3) | async-done | bytes 3145760 | tf_op jit(solution)/shard_map/all_to_all | solution.py:243
  370.0 34.5 %reduce-scatter.8.cloned.1.call-done = bf16[128,768]{1,0:T(8,128)(2,1)} async-done(((bf16[1024,768]{1,0:T(8,128)(2,1)}), bf16[128,768]{1,0:T(8,128)(2,1)}) %reduce-scatter.8.cloned.1.call-update) | async-done | bytes 196624 | tf_op jit(solution)/shard_map/reduce_scatter | solution.py:259
  (133 shorter events, 62.7 us)
Async XLA Ops:
  7.2 51.7 %reduce-scatter.4.cloned.1.call-start = ((), (), s32[]{:S(2)}) async-start(), calls=%async_computation.7 | async-start | bytes 3932160 | tf_op jit(solution)/shard_map/reduce_scatter | solution.py:169
  12.1 46.8 %copy-start.12 = (bf16[128,1536]{1,0:T(8,128)(2,1)S(1)}, bf16[128,1536]{1,0:T(8,128)(2,1)}, u32[]{:S(2)}) copy-start(bf16[128,1536]{1,0:T(8,128)(2,1)} %param.14) | copy-start | bytes 1179652
  12.1 48.1 %copy-start.14 = (f32[1536]{0:T(1024)S(1)}, f32[1536]{0:T(1024)}, u32[]{:S(2)}) copy-start(f32[1536]{0:T(1024)} %param.15) | copy-start | bytes 18436
  12.1 104.5 %all-gather.2.cloned.1.call-start = ((), (), s32[]{:S(2)}) async-start(), calls=%async_computation.8 | async-start | bytes 3538944 | tf_op jit(solution)/shard_map/all_gather | solution.py:180
  82.1 4.7 %copy-start.4 = (bf16[384,512]{1,0:T(8,128)(2,1)S(1)}, bf16[384,512]{1,0:T(8,128)(2,1)}, u32[]{:S(2)}) copy-start(bf16[384,512]{1,0:T(8,128)(2,1)} %reshape_squeeze.60) | copy-start | bytes 1179652
  82.1 4.7 %copy-start.6 = (bf16[192,512]{1,0:T(8,128)(2,1)S(1)}, bf16[192,512]{1,0:T(8,128)(2,1)}, u32[]{:S(2)}) copy-start(bf16[192,512]{1,0:T(8,128)(2,1)} %reshape_squeeze.57) | copy-start | bytes 589828
  82.1 4.7 %copy-start.7 = (bf16[192,512]{1,0:T(8,128)(2,1)S(1)}, bf16[192,512]{1,0:T(8,128)(2,1)}, u32[]{:S(2)}) copy-start(bf16[192,512]{1,0:T(8,128)(2,1)} %reshape_squeeze.62) | copy-start | bytes 589828
  82.1 4.7 %copy-start.8 = (bf16[192,512]{1,0:T(8,128)(2,1)S(1)}, bf16[192,512]{1,0:T(8,128)(2,1)}, u32[]{:S(2)}) copy-start(bf16[192,512]{1,0:T(8,128)(2,1)} %reshape_squeeze.61) | copy-start | bytes 589828
  82.2 4.7 %copy-start.9 = (bf16[192,512]{1,0:T(8,128)(2,1)S(1)}, bf16[192,512]{1,0:T(8,128)(2,1)}, u32[]{:S(2)}) copy-start(bf16[192,512]{1,0:T(8,128)(2,1)} %reshape_squeeze.58) | copy-start | bytes 589828
  90.2 5.4 %copy-start.17 = (s32[128,8]{0,1:T(8,128)S(1)}, s32[128,8]{0,1:T(8,128)}, u32[]{:S(2)}) copy-start(s32[128,8]{0,1:T(8,128)} %param.19) | copy-start | bytes 12292
  90.2 5.4 %copy-start.18 = (s32[128,8]{0,1:T(8,128)S(1)}, s32[128,8]{0,1:T(8,128)}, u32[]{:S(2)}) copy-start(s32[128,8]{0,1:T(8,128)} %param.18) | copy-start | bytes 12292
  90.2 19.9 %copy-start.16 = (s32[48]{0:T(128)S(1)}, s32[48]{0:T(128)}, u32[]{:S(2)}) copy-start(s32[48]{0:T(128)} %param.20) | copy-start | bytes 580
  90.2 75.2 %all-to-all-start.1 = ((bf16[4,1536,512]{2,1,0:T(8,128)(2,1)}), bf16[4,1536,512]{2,1,0:T(8,128)(2,1)}, u32[]{:S(2)}, u32[]{:S(2)}) async-start(bf16[4,1536,512]{2,1,0:T(8,128)(2,1)} %pad_maximum_fusion.1), calls=%async_computation.2 | async-start | bytes 12582912 | tf_op jit(solution)/shard_map/all_to_all | solution.py:125
  124.2 46.7 %copy-start.11 = (bf16[128,1536]{1,0:T(8,128)(2,1)S(1)}, bf16[128,1536]{1,0:T(8,128)(2,1)}, u32[]{:S(2)}) copy-start(bf16[128,1536]{1,0:T(8,128)(2,1)} %get-tuple-element.36) | copy-start | bytes 1179652
  165.4 99.2 %all-to-all-start = ((bf16[4,2,8,32,1536]{4,3,2,1,0:T(8,128)(2,1)}), bf16[4,2,8,32,1536]{4,3,2,1,0:T(8,128)(2,1)}, u32[]{:S(2)}, u32[]{:S(2)}) async-start(bf16[4,2,8,32,1536]{4,3,2,1,0:T(8,128)(2,1)} %pad_maximum_fusion), calls=%async_computation.1 | async-start | bytes 12582912 | tf_op jit(solution)/shard_map/all_to_all | solution.py:208
  170.9 77.5 %collective-permute-start = (bf16[128,1536]{1,0:T(8,128)(2,1)S(1)}, bf16[128,1536]{1,0:T(8,128)(2,1)S(1)}, u32[]{:S(2)}, u32[]{:S(2)}) collective-permute-start(bf16[128,1536]{1,0:T(8,128)(2,1)S(1)} %copy-done.11), channel_id=1, source_target_pairs={{8,0},{0,8},{24,16},{16,24},{9,1},{1,9},{25,17},{17,25},{10,2},{2,... | collective-permute-start | bytes 1179656 | tf_op jit(solution)/shard_map/ppermute | solution.py:159
  264.6 3.7 copy-start.2
  280.5 4.8 %copy-start.13 = (bf16[1536,40]{0,1:T(8,128)(2,1)S(1)}, bf16[1536,40]{0,1:T(8,128)(2,1)}, u32[]{:S(2)}) copy-start(bf16[1536,40]{0,1:T(8,128)(2,1)} %param.17) | copy-start | bytes 368644
  280.5 39.6 %all-to-all-start.2 = ((bf16[4,2,8,32,768]{4,3,2,1,0:T(8,128)(2,1)}), bf16[4,2,8,32,768]{4,3,2,1,0:T(8,128)(2,1)}, u32[]{:S(2)}, u32[]{:S(2)}) async-start(bf16[4,2,8,32,768]{4,3,2,1,0:T(8,128)(2,1)} %get-tuple-element.8), calls=%async_computation.3 | async-start | bytes 6291456 | tf_op jit(solution)/shard_map/all_to_all | solution.py:243
  320.2 40.3 %all-to-all-start.3 = ((bf16[4,2,8,32,768]{4,3,2,1,0:T(8,128)(2,1)}), bf16[4,2,8,32,768]{4,3,2,1,0:T(8,128)(2,1)}, u32[]{:S(2)}, u32[]{:S(2)}) async-start(bf16[4,2,8,32,768]{4,3,2,1,0:T(8,128)(2,1)} %get-tuple-element.9), calls=%async_computation.5 | async-start | bytes 6291456 | tf_op jit(solution)/shard_map/all_to_all | solution.py:243
  324.8 45.2 %reduce-scatter.6.cloned.1.call-start = ((), (), s32[]{:S(2)}) async-start(), calls=%async_computation.9 | async-start | bytes 1769472 | tf_op jit(solution)/shard_map/reduce_scatter | solution.py:259
  334.3 70.2 %reduce-scatter.8.cloned.1.call-start = ((), (), s32[]{:S(2)}) async-start(), calls=%async_computation.10 | async-start | bytes 1769472 | tf_op jit(solution)/shard_map/reduce_scatter | solution.py:259
  367.9 38.9 %copy-start.1 = (bf16[384,1536]{1,0:T(8,128)(2,1)S(1)}, bf16[384,1536]{1,0:T(8,128)(2,1)}, u32[]{:S(2)}) copy-start(bf16[384,1536]{1,0:T(8,128)(2,1)} %param.13) | copy-start | bytes 3538948
  369.7 36.1 %copy-start.15 = (f32[1536]{0:T(1024)S(1)}, f32[1536]{0:T(1024)}, u32[]{:S(2)}) copy-start(f32[1536]{0:T(1024)} %param.16) | copy-start | bytes 18436
  (5 other events, 10.1 us)
Sparse Core Ops, SparseCore 0:
  12.2 46.6 reduce-scatter.3
  61.3 38.2 all-gather.1
  334.4 35.5 reduce-scatter.5
  372.2 32.3 reduce-scatter.7
where the time goes:
time: 415 us; the launch traced here: 413 us
  waiting for transfers between devices  255 us (61%)
  local copies, waits for them, and re-layouts  54.7 us (13%)
  other arithmetic  28.2 us (7%)
  matrix products  24.2 us (6%)
  starting transfers between devices  22.4 us (5%)
  between operations  14.4 us (3%)
  blocking collectives  14.2 us (3%)
    ppermute x1, waiting for transfers between devices, on_device_body(): held.append(lax.ppermute(sent, 'dp', pairs))  75.7 us
    all_to_all x2, waiting for transfers between devices, on_device_body(): y_recv = lax.all_to_all(y_send[..., cols], 'dp', 0, 0, tiled=True)  56.6 us
    reduce_scatter x1, waiting for transfers between devices, on_device_body(): lax.psum_scatter(jnp.dot(flat_context, w_proj, preferred_element_type=jnp...  46.7 us
    all_to_all x1, waiting for transfers between devices, on_device_body(): lax.all_to_all(jnp.stack(weight_parts), 'dp', 0, 0, tiled=True)  41.2 us
    reduce_scatter x2, waiting for transfers between devices, on_device_body(): lax.psum_scatter(partial.reshape(n_exp * tok_rows, piece_width).astype(jn...  34.8 us
    all_gather x1, blocking collectives, on_device_body(): lax.all_gather(jnp.concatenate([expert_ids, replica_pick], axis=1), 'expe...  14.2 us
    another operation x16, local copies, waits for them, and re-layouts, as_rows(): return piece.reshape(-1, lane_width)  13.1 us
    unnamed x49, local copies, waits for them, and re-layouts  9.83 us
  transfers between devices with their start and end apart: 9, of which 7 were waited for; matrix products, arithmetic and copies ran while one was open for 20% of the time, Pallas kernels for 0%

commit v1 on v0

--- a/solution.py
+++ b/solution.py
@@ -15,11 +15,10 @@
     return widened * lax.rsqrt(jnp.mean(widened * widened, axis=-1, keepdims=True) + 1e-06) * gain
 
 
-def route_rows(normed, w_router, expert_ids, replica_pick, slot_expert, cap_blocks, cap_unit):
+def route_rows(logits, w_router, expert_ids, replica_pick, slot_expert, cap_blocks, cap_unit):
     blocks, row_count, topk_all = expert_ids.shape
     experts_all = w_router.shape[1]
     slots_all = slot_expert.shape[0]
-    logits = jnp.dot(normed, w_router, preferred_element_type=jnp.float32)
     logits = logits.reshape(blocks, row_count, experts_all)
     expert_axis = jnp.arange(experts_all)
     one_hot = expert_ids[..., None] == expert_axis
@@ -122,8 +121,10 @@
             if not paired:
                 pieces.append(as_rows(w_out[s]))
         weight_parts.append(jnp.concatenate(pieces, axis=0))
-    weight_recv = lax.all_to_all(jnp.stack(weight_parts), "dp", 0, 0, tiled=True)
+    weight_send = jnp.stack(weight_parts)
+    weight_recv = lax.all_to_all(weight_send, "dp", 0, 0, tiled=True)
     offset = 0
+
 
     def take(shape):
         nonlocal offset
@@ -178,8 +179,9 @@
     normed = rms_scale(hidden_state, gain_first).astype(jnp.bfloat16)
 
     normed_all = lax.all_gather(normed, "expert", axis=0, tiled=True)
+    logits = jnp.dot(normed_all, w_router, preferred_element_type=jnp.float32)
     gates, target_slot, position, retained = route_rows(
-        normed_all,
+        logits,
         w_router,
         ids_all[:, :, :topk_all],
         ids_all[:, :, topk_all:],

time: 415 us -> 415 us (level)
  no operation moved by 1% of the time
where the time goes in v1:
time: 415 us; the launch traced here: 413 us
  waiting for transfers between devices  255 us (61%)
  local copies, waits for them, and re-layouts  54.7 us (13%)
  other arithmetic  28.2 us (7%)
  matrix products  24.2 us (6%)
  starting transfers between devices  22.4 us (5%)
  between operations  14.4 us (3%)
  blocking collectives  14.2 us (3%)
    ppermute x1, waiting for transfers between devices, on_device_body(): held.append(lax.ppermute(sent, 'dp', pairs))  75.7 us
    all_to_all x2, waiting for transfers between devices, on_device_body(): y_recv = lax.all_to_all(y_send[..., cols], 'dp', 0, 0, tiled=True)  56.6 us
    reduce_scatter x1, waiting for transfers between devices, on_device_body(): lax.psum_scatter(jnp.dot(flat_context, w_proj, preferred_element_type=jnp...  46.7 us
    all_to_all x1, waiting for transfers between devices, on_device_body(): weight_recv = lax.all_to_all(weight_send, 'dp', 0, 0, tiled=True)  41.2 us
    reduce_scatter x2, waiting for transfers between devices, on_device_body(): lax.psum_scatter(partial.reshape(n_exp * tok_rows, piece_width).astype(jn...  34.8 us
    all_gather x1, blocking collectives, on_device_body(): lax.all_gather(jnp.concatenate([expert_ids, replica_pick], axis=1), 'expe...  14.2 us
    another operation x16, local copies, waits for them, and re-layouts, as_rows(): return piece.reshape(-1, lane_width)  13.1 us
    unnamed x49, local copies, waits for them, and re-layouts  9.83 us
  transfers between devices with their start and end apart: 9, of which 7 were waited for; matrix products, arithmetic and copies ran while one was open for 20% of the time, Pallas kernels for 0%

profile of v1, /device:TPU:0, one launch (start us, length us, event | category | flops | bytes accessed | tf_op | source)
XLA Modules:
  0.0 413.3 jit_solution(11537969740410243941)
XLA Ops:
  8.4 3.6 fusion.76
  12.1 46.7 %reduce-scatter.4.cloned.1.call-done = f32[128,1536]{1,0:T(8,128)} async-done(((f32[512,1536]{1,0:T(8,128)}), f32[128,1536]{1,0:T(8,128)}) %reduce-scatter.4.cloned.1.call-update) | async-done | bytes 786448 | tf_op jit(solution)/shard_map/reduce_scatter | solution.py:170
  68.7 2.8 fusion.74
  74.5 3.5 fusion.72
  82.2 4.6 %maximum_bitcast_fusion.3 = (bf16[1,1536,512]{2,1,0:T(8,128)(2,1)S(1)}, bf16[1,1536,512]{2,1,0:T(8,128)(2,1)S(1)}) fusion(bf16[192,512]{1,0:T(8,128)(2,1)} %reshape_squeeze.66, bf16[192,512]{1,0:T(8,128)(2,1)} %reshape_squeeze.65, bf16[384,512]{1,0:T(8,128)(2,1)} %reshape_squeeze.64, bf16[768,512]{1,0:T(8,128)(2,1)} %reshape_squeeze.63, ...), kind=kLoop, calls=%fused_computation.28 | loop fusion | flops 12582912 | bytes 6291456 | tf_op jit(solution)/shard_map/stack | solution.py:124
  87.1 3.1 pad_maximum_fusion.1
  90.2 5.4 %all-to-all-start.1 = ((bf16[4,1536,512]{2,1,0:T(8,128)(2,1)}), bf16[4,1536,512]{2,1,0:T(8,128)(2,1)}, u32[]{:S(2)}, u32[]{:S(2)}) async-start(bf16[4,1536,512]{2,1,0:T(8,128)(2,1)} %pad_maximum_fusion.1), calls=%async_computation.2 | async-start | bytes 12582912 | tf_op jit(solution)/shard_map/all_to_all | solution.py:125
  95.6 14.2 %all_gather.6 = s32[1024,16]{0,1:T(8,128)S(1)} all-gather(s32[128,16]{0,1:T(8,128)S(1)} %pad_add_fusion), channel_id=1, replica_groups=mesh['dp'=4,'expert'=8] {'expert'}, dimensions={0}, use_global_device_ids=true | all-gather | bytes 73728 | tf_op jit(solution)/shard_map/all_gather | solution.py:165
  116.5 3.3 convolution_convert_fusion
  120.9 3.4 pad_maximum_fusion
  124.2 41.2 %all-to-all-done.1 = bf16[4,1536,512]{2,1,0:T(8,128)(2,1)} async-done(((bf16[4,1536,512]{2,1,0:T(8,128)(2,1)}), bf16[4,1536,512]{2,1,0:T(8,128)(2,1)}, u32[]{:S(2)}, u32[]{:S(2)}) %all-to-all-start.1) | async-done | bytes 6291488 | tf_op jit(solution)/shard_map/all_to_all | solution.py:125
  165.4 5.5 %all-to-all-start = ((bf16[4,2,8,32,1536]{4,3,2,1,0:T(8,128)(2,1)}), bf16[4,2,8,32,1536]{4,3,2,1,0:T(8,128)(2,1)}, u32[]{:S(2)}, u32[]{:S(2)}) async-start(bf16[4,2,8,32,1536]{4,3,2,1,0:T(8,128)(2,1)} %pad_maximum_fusion), calls=%async_computation.1 | async-start | bytes 12582912 | tf_op jit(solution)/shard_map/all_to_all | solution.py:210
  172.7 75.7 %collective-permute-done = bf16[128,1536]{1,0:T(8,128)(2,1)S(1)} collective-permute-done((bf16[128,1536]{1,0:T(8,128)(2,1)S(1)}, bf16[128,1536]{1,0:T(8,128)(2,1)S(1)}, u32[]{:S(2)}, u32[]{:S(2)}) %collective-permute-start) | collective-permute-done | bytes 393248 | tf_op jit(solution)/shard_map/ppermute | solution.py:160
  253.0 3.8 slice.219
  256.9 5.7 %reshape_reshape.6 = bf16[1536,1024]{1,0:T(8,128)(2,1)} reshape(bf16[4,768,512]{2,1,0:T(8,128)(2,1)} %slice.219) | data formatting | bytes 6291456 | tf_op jit(solution)/shard_map/reshape;reshape | solution.py:138
  264.6 3.4 fusion.70
  268.4 3.4 fusion.77
  277.0 3.5 fusion.69
  280.5 4.8 %all-to-all-start.2 = ((bf16[4,2,8,32,768]{4,3,2,1,0:T(8,128)(2,1)}), bf16[4,2,8,32,768]{4,3,2,1,0:T(8,128)(2,1)}, u32[]{:S(2)}, u32[]{:S(2)}) async-start(bf16[4,2,8,32,768]{4,3,2,1,0:T(8,128)(2,1)} %get-tuple-element.8), calls=%async_computation.3 | async-start | bytes 6291456 | tf_op jit(solution)/shard_map/all_to_all | solution.py:245
  285.3 2.9 convolution_bitcast_fusion
  289.7 30.5 %all-to-all-done.2 = bf16[4,2,8,32,768]{4,3,2,1,0:T(8,128)(2,1)} async-done(((bf16[4,2,8,32,768]{4,3,2,1,0:T(8,128)(2,1)}), bf16[4,2,8,32,768]{4,3,2,1,0:T(8,128)(2,1)}, u32[]{:S(2)}, u32[]{:S(2)}) %all-to-all-start.2) | async-done | bytes 3145760 | tf_op jit(solution)/shard_map/all_to_all | solution.py:245
  320.2 4.6 %all-to-all-start.3 = ((bf16[4,2,8,32,768]{4,3,2,1,0:T(8,128)(2,1)}), bf16[4,2,8,32,768]{4,3,2,1,0:T(8,128)(2,1)}, u32[]{:S(2)}, u32[]{:S(2)}) async-start(bf16[4,2,8,32,768]{4,3,2,1,0:T(8,128)(2,1)} %get-tuple-element.9), calls=%async_computation.5 | async-start | bytes 6291456 | tf_op jit(solution)/shard_map/all_to_all | solution.py:245
  334.4 26.1 %all-to-all-done.3 = bf16[4,2,8,32,768]{4,3,2,1,0:T(8,128)(2,1)} async-done(((bf16[4,2,8,32,768]{4,3,2,1,0:T(8,128)(2,1)}), bf16[4,2,8,32,768]{4,3,2,1,0:T(8,128)(2,1)}, u32[]{:S(2)}, u32[]{:S(2)}) %all-to-all-start.3) | async-done | bytes 3145760 | tf_op jit(solution)/shard_map/all_to_all | solution.py:245
  370.0 34.5 %reduce-scatter.8.cloned.1.call-done = bf16[128,768]{1,0:T(8,128)(2,1)} async-done(((bf16[1024,768]{1,0:T(8,128)(2,1)}), bf16[128,768]{1,0:T(8,128)(2,1)}) %reduce-scatter.8.cloned.1.call-update) | async-done | bytes 196624 | tf_op jit(solution)/shard_map/reduce_scatter | solution.py:261
  (133 shorter events, 62.7 us)
Async XLA Ops:
  7.2 51.7 %reduce-scatter.4.cloned.1.call-start = ((), (), s32[]{:S(2)}) async-start(), calls=%async_computation.7 | async-start | bytes 3932160 | tf_op jit(solution)/shard_map/reduce_scatter | solution.py:170
  12.1 46.8 %copy-start.12 = (bf16[128,1536]{1,0:T(8,128)(2,1)S(1)}, bf16[128,1536]{1,0:T(8,128)(2,1)}, u32[]{:S(2)}) copy-start(bf16[128,1536]{1,0:T(8,128)(2,1)} %param.14) | copy-start | bytes 1179652
  12.1 48.1 %copy-start.14 = (f32[1536]{0:T(1024)S(1)}, f32[1536]{0:T(1024)}, u32[]{:S(2)}) copy-start(f32[1536]{0:T(1024)} %param.15) | copy-start | bytes 18436
  12.1 104.5 %all-gather.2.cloned.1.call-start = ((), (), s32[]{:S(2)}) async-start(), calls=%async_computation.8 | async-start | bytes 3538944 | tf_op jit(solution)/shard_map/all_gather | solution.py:181
  82.1 4.7 %copy-start.4 = (bf16[384,512]{1,0:T(8,128)(2,1)S(1)}, bf16[384,512]{1,0:T(8,128)(2,1)}, u32[]{:S(2)}) copy-start(bf16[384,512]{1,0:T(8,128)(2,1)} %reshape_squeeze.60) | copy-start | bytes 1179652
  82.1 4.7 %copy-start.6 = (bf16[192,512]{1,0:T(8,128)(2,1)S(1)}, bf16[192,512]{1,0:T(8,128)(2,1)}, u32[]{:S(2)}) copy-start(bf16[192,512]{1,0:T(8,128)(2,1)} %reshape_squeeze.57) | copy-start | bytes 589828
  82.1 4.7 %copy-start.7 = (bf16[192,512]{1,0:T(8,128)(2,1)S(1)}, bf16[192,512]{1,0:T(8,128)(2,1)}, u32[]{:S(2)}) copy-start(bf16[192,512]{1,0:T(8,128)(2,1)} %reshape_squeeze.62) | copy-start | bytes 589828
  82.1 4.7 %copy-start.8 = (bf16[192,512]{1,0:T(8,128)(2,1)S(1)}, bf16[192,512]{1,0:T(8,128)(2,1)}, u32[]{:S(2)}) copy-start(bf16[192,512]{1,0:T(8,128)(2,1)} %reshape_squeeze.61) | copy-start | bytes 589828
  82.2 4.7 %copy-start.9 = (bf16[192,512]{1,0:T(8,128)(2,1)S(1)}, bf16[192,512]{1,0:T(8,128)(2,1)}, u32[]{:S(2)}) copy-start(bf16[192,512]{1,0:T(8,128)(2,1)} %reshape_squeeze.58) | copy-start | bytes 589828
  90.2 5.4 %copy-start.17 = (s32[128,8]{0,1:T(8,128)S(1)}, s32[128,8]{0,1:T(8,128)}, u32[]{:S(2)}) copy-start(s32[128,8]{0,1:T(8,128)} %param.19) | copy-start | bytes 12292
  90.2 5.4 %copy-start.18 = (s32[128,8]{0,1:T(8,128)S(1)}, s32[128,8]{0,1:T(8,128)}, u32[]{:S(2)}) copy-start(s32[128,8]{0,1:T(8,128)} %param.18) | copy-start | bytes 12292
  90.2 19.9 %copy-start.16 = (s32[48]{0:T(128)S(1)}, s32[48]{0:T(128)}, u32[]{:S(2)}) copy-start(s32[48]{0:T(128)} %param.20) | copy-start | bytes 580
  90.2 75.2 %all-to-all-start.1 = ((bf16[4,1536,512]{2,1,0:T(8,128)(2,1)}), bf16[4,1536,512]{2,1,0:T(8,128)(2,1)}, u32[]{:S(2)}, u32[]{:S(2)}) async-start(bf16[4,1536,512]{2,1,0:T(8,128)(2,1)} %pad_maximum_fusion.1), calls=%async_computation.2 | async-start | bytes 12582912 | tf_op jit(solution)/shard_map/all_to_all | solution.py:125
  124.2 46.7 %copy-start.11 = (bf16[128,1536]{1,0:T(8,128)(2,1)S(1)}, bf16[128,1536]{1,0:T(8,128)(2,1)}, u32[]{:S(2)}) copy-start(bf16[128,1536]{1,0:T(8,128)(2,1)} %get-tuple-element.36) | copy-start | bytes 1179652
  165.4 99.2 %all-to-all-start = ((bf16[4,2,8,32,1536]{4,3,2,1,0:T(8,128)(2,1)}), bf16[4,2,8,32,1536]{4,3,2,1,0:T(8,128)(2,1)}, u32[]{:S(2)}, u32[]{:S(2)}) async-start(bf16[4,2,8,32,1536]{4,3,2,1,0:T(8,128)(2,1)} %pad_maximum_fusion), calls=%async_computation.1 | async-start | bytes 12582912 | tf_op jit(solution)/shard_map/all_to_all | solution.py:210
  170.9 77.5 %collective-permute-start = (bf16[128,1536]{1,0:T(8,128)(2,1)S(1)}, bf16[128,1536]{1,0:T(8,128)(2,1)S(1)}, u32[]{:S(2)}, u32[]{:S(2)}) collective-permute-start(bf16[128,1536]{1,0:T(8,128)(2,1)S(1)} %copy-done.11), channel_id=1, source_target_pairs={{8,0},{0,8},{24,16},{16,24},{9,1},{1,9},{25,17},{17,25},{10,2},{2,... | collective-permute-start | bytes 1179656 | tf_op jit(solution)/shard_map/ppermute | solution.py:160
  264.6 3.7 copy-start.2
  280.5 4.8 %copy-start.13 = (bf16[1536,40]{0,1:T(8,128)(2,1)S(1)}, bf16[1536,40]{0,1:T(8,128)(2,1)}, u32[]{:S(2)}) copy-start(bf16[1536,40]{0,1:T(8,128)(2,1)} %param.17) | copy-start | bytes 368644
  280.5 39.6 %all-to-all-start.2 = ((bf16[4,2,8,32,768]{4,3,2,1,0:T(8,128)(2,1)}), bf16[4,2,8,32,768]{4,3,2,1,0:T(8,128)(2,1)}, u32[]{:S(2)}, u32[]{:S(2)}) async-start(bf16[4,2,8,32,768]{4,3,2,1,0:T(8,128)(2,1)} %get-tuple-element.8), calls=%async_computation.3 | async-start | bytes 6291456 | tf_op jit(solution)/shard_map/all_to_all | solution.py:245
  320.2 40.3 %all-to-all-start.3 = ((bf16[4,2,8,32,768]{4,3,2,1,0:T(8,128)(2,1)}), bf16[4,2,8,32,768]{4,3,2,1,0:T(8,128)(2,1)}, u32[]{:S(2)}, u32[]{:S(2)}) async-start(bf16[4,2,8,32,768]{4,3,2,1,0:T(8,128)(2,1)} %get-tuple-element.9), calls=%async_computation.5 | async-start | bytes 6291456 | tf_op jit(solution)/shard_map/all_to_all | solution.py:245
  324.8 45.2 %reduce-scatter.6.cloned.1.call-start = ((), (), s32[]{:S(2)}) async-start(), calls=%async_computation.9 | async-start | bytes 1769472 | tf_op jit(solution)/shard_map/reduce_scatter | solution.py:261
  334.3 70.2 %reduce-scatter.8.cloned.1.call-start = ((), (), s32[]{:S(2)}) async-start(), calls=%async_computation.10 | async-start | bytes 1769472 | tf_op jit(solution)/shard_map/reduce_scatter | solution.py:261
  367.9 38.9 %copy-start.1 = (bf16[384,1536]{1,0:T(8,128)(2,1)S(1)}, bf16[384,1536]{1,0:T(8,128)(2,1)}, u32[]{:S(2)}) copy-start(bf16[384,1536]{1,0:T(8,128)(2,1)} %param.13) | copy-start | bytes 3538948
  369.7 36.1 %copy-start.15 = (f32[1536]{0:T(1024)S(1)}, f32[1536]{0:T(1024)}, u32[]{:S(2)}) copy-start(f32[1536]{0:T(1024)} %param.16) | copy-start | bytes 18436
  (5 other events, 10.1 us)
Sparse Core Ops, SparseCore 0:
  12.2 46.6 reduce-scatter.3
  61.3 38.2 all-gather.1
  334.4 35.5 reduce-scatter.5
  372.2 32.3 reduce-scatter.7

commit v2 on v1

--- a/solution.py
+++ b/solution.py
@@ -167,12 +167,11 @@
     ).reshape(n_exp, tok_rows, 2 * topk_all)
 
     flat_context = context.reshape(-1, context.shape[3])
-    attended = lax.psum_scatter(
-        jnp.dot(flat_context, w_proj, preferred_element_type=jnp.float32),
-        "dp",
-        scatter_dimension=0,
-        tiled=True,
-    )
+    head_parts = jnp.dot(flat_context, w_proj, preferred_element_type=jnp.float32)
+    head_parts = lax.all_to_all(
+        head_parts.reshape(n_dp, tok_rows, model_width), "dp", 0, 0, tiled=True
+    )
+    attended = jnp.sum(head_parts, axis=0)
     hidden_state = (residual.astype(jnp.float32) + attended.astype(jnp.float32)).astype(
         jnp.bfloat16
     )

time: 415 us -> 408 us (0.983)
  waiting for transfers between devices: 255 us -> 208 us
  blocking collectives: 14.2 us -> 56.1 us
    reduce_scatter x1 -> x0, waiting for transfers between devices: 46.7 us -> none  [on_device_body(): lax.psum_scatter(jnp.dot(flat_context, w_proj, preferred_element_type=jnp...]
    all_to_all x0 -> x1, blocking collectives: none -> 41.7 us  [on_device_body(): lax.all_to_all(head_parts.reshape(n_dp, tok_rows, model_width), 'dp', 0,...]
  transfers between devices with their start and end apart: 9 -> 8, of which waited for: 7 -> 6; matrix products, arithmetic and copies ran while one was open for 20% -> 20% of each run, Pallas kernels for 0% -> 0%
where the time goes in v2:
time: 408 us; the launch traced here: 407 us
  waiting for transfers between devices  208 us (51%)
  blocking collectives  56.1 us (14%)
  local copies, waits for them, and re-layouts  54.7 us (13%)
  other arithmetic  29.4 us (7%)
  matrix products  22.5 us (6%)
  starting transfers between devices  22.4 us (5%)
  between operations  14.4 us (4%)
    ppermute x1, waiting for transfers between devices, on_device_body(): held.append(lax.ppermute(sent, 'dp', pairs))  75.7 us
    all_to_all x2, waiting for transfers between devices, on_device_body(): y_recv = lax.all_to_all(y_send[..., cols], 'dp', 0, 0, tiled=True)  56.6 us
    all_to_all x1, blocking collectives, on_device_body(): lax.all_to_all(head_parts.reshape(n_dp, tok_rows, model_width), 'dp', 0,...  41.7 us
    all_to_all x1, waiting for transfers between devices, on_device_body(): weight_recv = lax.all_to_all(weight_send, 'dp', 0, 0, tiled=True)  39.8 us
    reduce_scatter x2, waiting for transfers between devices, on_device_body(): lax.psum_scatter(partial.reshape(n_exp * tok_rows, piece_width).astype(jn...  35.3 us
    all_gather x1, blocking collectives, on_device_body(): lax.all_gather(jnp.concatenate([expert_ids, replica_pick], axis=1), 'expe...  14.4 us
    another operation x16, local copies, waits for them, and re-layouts, as_rows(): return piece.reshape(-1, lane_width)  13.1 us
    unnamed x49, local copies, waits for them, and re-layouts  9.82 us
  transfers between devices with their start and end apart: 8, of which 6 were waited for; matrix products, arithmetic and copies ran while one was open for 20% of the time, Pallas kernels for 0%

profile of v2, /device:TPU:0, one launch (start us, length us, event | category | flops | bytes accessed | tf_op | source)
XLA Modules:
  0.0 407.0 jit_solution(16793730431847304206)
XLA Ops:
  10.4 41.7 %all_to_all.25 = f32[4,128,1536]{2,1,0:T(8,128)} all-to-all(f32[4,128,1536]{2,1,0:T(8,128)S(1)} %fusion.18), channel_id=1, replica_groups=mesh['dp'=4,'expert'=8] {'dp'}, dimensions={0} | all-to-all | bytes 6291456 | tf_op jit(solution)/shard_map/all_to_all | solution.py:171
  52.1 2.2 reduce_sum.108
  63.1 2.7 fusion.77
  68.9 3.5 fusion.75
  76.5 4.6 %maximum_bitcast_fusion.3 = (bf16[1,1536,512]{2,1,0:T(8,128)(2,1)S(1)}, bf16[1,1536,512]{2,1,0:T(8,128)(2,1)S(1)}) fusion(bf16[192,512]{1,0:T(8,128)(2,1)} %reshape_squeeze.66, bf16[192,512]{1,0:T(8,128)(2,1)} %reshape_squeeze.65, bf16[384,512]{1,0:T(8,128)(2,1)} %reshape_squeeze.64, bf16[768,512]{1,0:T(8,128)(2,1)} %reshape_squeeze.63, ...), kind=kLoop, calls=%fused_computation.28 | loop fusion | flops 12582912 | bytes 6291456 | tf_op jit(solution)/shard_map/stack | solution.py:124
  81.5 3.2 pad_maximum_fusion.1
  84.7 5.4 %all-to-all-start.2 = ((bf16[4,1536,512]{2,1,0:T(8,128)(2,1)}), bf16[4,1536,512]{2,1,0:T(8,128)(2,1)}, u32[]{:S(2)}, u32[]{:S(2)}) async-start(bf16[4,1536,512]{2,1,0:T(8,128)(2,1)} %pad_maximum_fusion.1), calls=%async_computation.2 | async-start | bytes 12582912 | tf_op jit(solution)/shard_map/all_to_all | solution.py:125
  90.1 14.4 %all_gather.6 = s32[1024,16]{0,1:T(8,128)S(1)} all-gather(s32[128,16]{0,1:T(8,128)S(1)} %pad_add_fusion), channel_id=1, replica_groups=mesh['dp'=4,'expert'=8] {'expert'}, dimensions={0}, use_global_device_ids=true | all-gather | bytes 73728 | tf_op jit(solution)/shard_map/all_gather | solution.py:165
  111.2 3.3 convolution_convert_fusion
  115.6 3.3 pad_maximum_fusion
  118.9 39.8 %all-to-all-done.2 = bf16[4,1536,512]{2,1,0:T(8,128)(2,1)} async-done(((bf16[4,1536,512]{2,1,0:T(8,128)(2,1)}), bf16[4,1536,512]{2,1,0:T(8,128)(2,1)}, u32[]{:S(2)}, u32[]{:S(2)}) %all-to-all-start.2) | async-done | bytes 6291488 | tf_op jit(solution)/shard_map/all_to_all | solution.py:125
  158.7 5.5 %all-to-all-start.1 = ((bf16[4,2,8,32,1536]{4,3,2,1,0:T(8,128)(2,1)}), bf16[4,2,8,32,1536]{4,3,2,1,0:T(8,128)(2,1)}, u32[]{:S(2)}, u32[]{:S(2)}) async-start(bf16[4,2,8,32,1536]{4,3,2,1,0:T(8,128)(2,1)} %pad_maximum_fusion), calls=%async_computation.1 | async-start | bytes 12582912 | tf_op jit(solution)/shard_map/all_to_all | solution.py:209
  165.9 75.7 %collective-permute-done = bf16[128,1536]{1,0:T(8,128)(2,1)S(1)} collective-permute-done((bf16[128,1536]{1,0:T(8,128)(2,1)S(1)}, bf16[128,1536]{1,0:T(8,128)(2,1)S(1)}, u32[]{:S(2)}, u32[]{:S(2)}) %collective-permute-start) | collective-permute-done | bytes 393248 | tf_op jit(solution)/shard_map/ppermute | solution.py:160
  246.3 3.8 slice.219
  250.1 5.7 %reshape_reshape.6 = bf16[1536,1024]{1,0:T(8,128)(2,1)} reshape(bf16[4,768,512]{2,1,0:T(8,128)(2,1)} %slice.219) | data formatting | bytes 6291456 | tf_op jit(solution)/shard_map/reshape;reshape | solution.py:138
  257.9 3.4 fusion.73
  261.6 3.4 fusion.79
  270.3 3.5 fusion.72
  273.7 4.8 %all-to-all-start.3 = ((bf16[4,2,8,32,768]{4,3,2,1,0:T(8,128)(2,1)}), bf16[4,2,8,32,768]{4,3,2,1,0:T(8,128)(2,1)}, u32[]{:S(2)}, u32[]{:S(2)}) async-start(bf16[4,2,8,32,768]{4,3,2,1,0:T(8,128)(2,1)} %get-tuple-element.8), calls=%async_computation.3 | async-start | bytes 6291456 | tf_op jit(solution)/shard_map/all_to_all | solution.py:244
  278.5 2.9 convolution_bitcast_fusion
  282.9 30.5 %all-to-all-done.3 = bf16[4,2,8,32,768]{4,3,2,1,0:T(8,128)(2,1)} async-done(((bf16[4,2,8,32,768]{4,3,2,1,0:T(8,128)(2,1)}), bf16[4,2,8,32,768]{4,3,2,1,0:T(8,128)(2,1)}, u32[]{:S(2)}, u32[]{:S(2)}) %all-to-all-start.3) | async-done | bytes 3145760 | tf_op jit(solution)/shard_map/all_to_all | solution.py:244
  313.4 4.6 %all-to-all-start.4 = ((bf16[4,2,8,32,768]{4,3,2,1,0:T(8,128)(2,1)}), bf16[4,2,8,32,768]{4,3,2,1,0:T(8,128)(2,1)}, u32[]{:S(2)}, u32[]{:S(2)}) async-start(bf16[4,2,8,32,768]{4,3,2,1,0:T(8,128)(2,1)} %get-tuple-element.9), calls=%async_computation.5 | async-start | bytes 6291456 | tf_op jit(solution)/shard_map/all_to_all | solution.py:244
  327.6 26.1 %all-to-all-done.4 = bf16[4,2,8,32,768]{4,3,2,1,0:T(8,128)(2,1)} async-done(((bf16[4,2,8,32,768]{4,3,2,1,0:T(8,128)(2,1)}), bf16[4,2,8,32,768]{4,3,2,1,0:T(8,128)(2,1)}, u32[]{:S(2)}, u32[]{:S(2)}) %all-to-all-start.4) | async-done | bytes 3145760 | tf_op jit(solution)/shard_map/all_to_all | solution.py:244
  363.5 34.8 %reduce-scatter.5.cloned.1.call-done = bf16[128,768]{1,0:T(8,128)(2,1)} async-done(((bf16[1024,768]{1,0:T(8,128)(2,1)}), bf16[128,768]{1,0:T(8,128)(2,1)}) %reduce-scatter.5.cloned.1.call-update) | async-done | bytes 196624 | tf_op jit(solution)/shard_map/reduce_scatter | solution.py:260
  (132 shorter events, 63.7 us)
Async XLA Ops:
  7.2 104.1 %all-gather.2.cloned.1.call-start = ((), (), s32[]{:S(2)}) async-start(), calls=%async_computation.7 | async-start | bytes 3538944 | tf_op jit(solution)/shard_map/all_gather | solution.py:180
  52.1 2.5 copy-start.14
  76.5 4.7 %copy-start.4 = (bf16[384,512]{1,0:T(8,128)(2,1)S(1)}, bf16[384,512]{1,0:T(8,128)(2,1)}, u32[]{:S(2)}) copy-start(bf16[384,512]{1,0:T(8,128)(2,1)} %reshape_squeeze.60) | copy-start | bytes 1179652
  76.5 4.7 %copy-start.6 = (bf16[192,512]{1,0:T(8,128)(2,1)S(1)}, bf16[192,512]{1,0:T(8,128)(2,1)}, u32[]{:S(2)}) copy-start(bf16[192,512]{1,0:T(8,128)(2,1)} %reshape_squeeze.57) | copy-start | bytes 589828
  76.5 4.7 %copy-start.7 = (bf16[192,512]{1,0:T(8,128)(2,1)S(1)}, bf16[192,512]{1,0:T(8,128)(2,1)}, u32[]{:S(2)}) copy-start(bf16[192,512]{1,0:T(8,128)(2,1)} %reshape_squeeze.62) | copy-start | bytes 589828
  76.5 4.7 %copy-start.8 = (bf16[192,512]{1,0:T(8,128)(2,1)S(1)}, bf16[192,512]{1,0:T(8,128)(2,1)}, u32[]{:S(2)}) copy-start(bf16[192,512]{1,0:T(8,128)(2,1)} %reshape_squeeze.61) | copy-start | bytes 589828
  76.5 4.7 %copy-start.9 = (bf16[192,512]{1,0:T(8,128)(2,1)S(1)}, bf16[192,512]{1,0:T(8,128)(2,1)}, u32[]{:S(2)}) copy-start(bf16[192,512]{1,0:T(8,128)(2,1)} %reshape_squeeze.58) | copy-start | bytes 589828
  84.6 5.4 %copy-start.17 = (s32[128,8]{0,1:T(8,128)S(1)}, s32[128,8]{0,1:T(8,128)}, u32[]{:S(2)}) copy-start(s32[128,8]{0,1:T(8,128)} %param.19) | copy-start | bytes 12292
  84.7 5.4 %copy-start.18 = (s32[128,8]{0,1:T(8,128)S(1)}, s32[128,8]{0,1:T(8,128)}, u32[]{:S(2)}) copy-start(s32[128,8]{0,1:T(8,128)} %param.18) | copy-start | bytes 12292
  84.7 20.1 %copy-start.16 = (s32[48]{0:T(128)S(1)}, s32[48]{0:T(128)}, u32[]{:S(2)}) copy-start(s32[48]{0:T(128)} %param.20) | copy-start | bytes 580
  84.7 74.0 %all-to-all-start.2 = ((bf16[4,1536,512]{2,1,0:T(8,128)(2,1)}), bf16[4,1536,512]{2,1,0:T(8,128)(2,1)}, u32[]{:S(2)}, u32[]{:S(2)}) async-start(bf16[4,1536,512]{2,1,0:T(8,128)(2,1)} %pad_maximum_fusion.1), calls=%async_computation.2 | async-start | bytes 12582912 | tf_op jit(solution)/shard_map/all_to_all | solution.py:125
  106.7 2.7 copy-start.19
  118.9 45.3 %copy-start.11 = (bf16[128,1536]{1,0:T(8,128)(2,1)S(1)}, bf16[128,1536]{1,0:T(8,128)(2,1)}, u32[]{:S(2)}) copy-start(bf16[128,1536]{1,0:T(8,128)(2,1)} %get-tuple-element.36) | copy-start | bytes 1179652
  158.7 99.2 %all-to-all-start.1 = ((bf16[4,2,8,32,1536]{4,3,2,1,0:T(8,128)(2,1)}), bf16[4,2,8,32,1536]{4,3,2,1,0:T(8,128)(2,1)}, u32[]{:S(2)}, u32[]{:S(2)}) async-start(bf16[4,2,8,32,1536]{4,3,2,1,0:T(8,128)(2,1)} %pad_maximum_fusion), calls=%async_computation.1 | async-start | bytes 12582912 | tf_op jit(solution)/shard_map/all_to_all | solution.py:209
  164.2 77.5 %collective-permute-start = (bf16[128,1536]{1,0:T(8,128)(2,1)S(1)}, bf16[128,1536]{1,0:T(8,128)(2,1)S(1)}, u32[]{:S(2)}, u32[]{:S(2)}) collective-permute-start(bf16[128,1536]{1,0:T(8,128)(2,1)S(1)} %copy-done.11), channel_id=1, source_target_pairs={{8,0},{0,8},{24,16},{16,24},{9,1},{1,9},{25,17},{17,25},{10,2},{2,... | collective-permute-start | bytes 1179656 | tf_op jit(solution)/shard_map/ppermute | solution.py:160
  257.8 3.7 copy-start.2
  261.6 3.4 copy-start.3
  273.7 4.8 %copy-start.13 = (bf16[1536,40]{0,1:T(8,128)(2,1)S(1)}, bf16[1536,40]{0,1:T(8,128)(2,1)}, u32[]{:S(2)}) copy-start(bf16[1536,40]{0,1:T(8,128)(2,1)} %param.17) | copy-start | bytes 368644
  273.7 39.6 %all-to-all-start.3 = ((bf16[4,2,8,32,768]{4,3,2,1,0:T(8,128)(2,1)}), bf16[4,2,8,32,768]{4,3,2,1,0:T(8,128)(2,1)}, u32[]{:S(2)}, u32[]{:S(2)}) async-start(bf16[4,2,8,32,768]{4,3,2,1,0:T(8,128)(2,1)} %get-tuple-element.8), calls=%async_computation.3 | async-start | bytes 6291456 | tf_op jit(solution)/shard_map/all_to_all | solution.py:244
  313.4 40.3 %all-to-all-start.4 = ((bf16[4,2,8,32,768]{4,3,2,1,0:T(8,128)(2,1)}), bf16[4,2,8,32,768]{4,3,2,1,0:T(8,128)(2,1)}, u32[]{:S(2)}, u32[]{:S(2)}) async-start(bf16[4,2,8,32,768]{4,3,2,1,0:T(8,128)(2,1)} %get-tuple-element.9), calls=%async_computation.5 | async-start | bytes 6291456 | tf_op jit(solution)/shard_map/all_to_all | solution.py:244
  318.0 45.5 %reduce-scatter.3.cloned.1.call-start = ((), (), s32[]{:S(2)}) async-start(), calls=%async_computation.8 | async-start | bytes 1769472 | tf_op jit(solution)/shard_map/reduce_scatter | solution.py:260
  327.5 70.8 %reduce-scatter.5.cloned.1.call-start = ((), (), s32[]{:S(2)}) async-start(), calls=%async_computation.9 | async-start | bytes 1769472 | tf_op jit(solution)/shard_map/reduce_scatter | solution.py:260
  361.1 39.4 %copy-start.1 = (bf16[384,1536]{1,0:T(8,128)(2,1)S(1)}, bf16[384,1536]{1,0:T(8,128)(2,1)}, u32[]{:S(2)}) copy-start(bf16[384,1536]{1,0:T(8,128)(2,1)} %param.13) | copy-start | bytes 3538948
  362.9 36.6 %copy-start.15 = (f32[1536]{0:T(1024)S(1)}, f32[1536]{0:T(1024)}, u32[]{:S(2)}) copy-start(f32[1536]{0:T(1024)} %param.16) | copy-start | bytes 18436
  (4 other events, 6.3 us)
Sparse Core Ops, SparseCore 0:
  55.6 37.9 all-gather.1
  327.6 35.7 reduce-scatter.2
  365.8 32.4 reduce-scatter.4

commit v3 on v2

--- a/solution.py
+++ b/solution.py
@@ -206,21 +206,28 @@
         x_parts.append(
             jnp.stack([slot_in[:, s] for s in owned_full[o]] + [slot_in[:, s] for s, _ in owned_part[o]])
         )
-    x_recv = lax.all_to_all(jnp.stack(x_parts), "dp", 0, 0, tiled=True)
-
-    unit_rows = n_dp * n_exp * CAP_MOST
-
-    def expert_rows(rows, w_up, w_down, width):
+    x_send = jnp.stack(x_parts)
+    src_pieces = 2 if n_exp % 2 == 0 else 1
+    src_width = n_exp // src_pieces
+    x_recvs = [
+        lax.all_to_all(x_send[:, :, p * src_width:(p + 1) * src_width], "dp", 0, 0, tiled=True)
+        for p in range(src_pieces)
+    ]
+
+    piece_rows = n_dp * src_width * CAP_MOST
+
+    def activate(rows, w_up, width):
         gate_up = jnp.dot(rows, w_up, preferred_element_type=jnp.float32)
-        activated = (jax.nn.silu(gate_up[:, :width]) * gate_up[:, width:]).astype(jnp.bfloat16)
-        return jnp.dot(activated, w_down, preferred_element_type=jnp.float32).astype(jnp.bfloat16)
-
-    outs = []
+        return (jax.nn.silu(gate_up[:, :width]) * gate_up[:, width:]).astype(jnp.bfloat16)
+
+    acts, downs = [], []
     for j in range(full):
-        rows = x_recv[:, j].reshape(unit_rows, model_width)
-        outs.append(expert_rows(rows, full_in[j], full_out[j], hidden_units))
+        acts.append([
+            activate(x_recv[:, j].reshape(piece_rows, model_width), full_in[j], hidden_units)
+            for x_recv in x_recvs
+        ])
+        downs.append(full_out[j])
     for i in range(halves):
-        rows = x_recv[:, full + i].reshape(unit_rows, model_width)
         if paired:
             w_down = part_out[i]
         else:
@@ -228,12 +235,29 @@
             w_down = lax.dynamic_slice_in_dim(
                 part_out[i], chunk_at * sources_per_chunk, sources_per_chunk, axis=0
             ).reshape(chunk_width, model_width)
-        outs.append(expert_rows(rows, part_in[i], w_down, chunk_width))
-    y_send = (
-        jnp.stack(outs)
-        .reshape(full + halves, n_dp, n_exp, CAP_MOST, model_width)
-        .transpose(1, 0, 2, 3, 4)
-    )
+        acts.append([
+            activate(
+                x_recv[:, full + i].reshape(piece_rows, model_width), part_in[i], chunk_width
+            )
+            for x_recv in x_recvs
+        ])
+        downs.append(w_down)
+
+    def returned_piece(cols):
+        outs = [
+            jnp.concatenate(
+                [
+                    jnp.dot(act, down[:, cols], preferred_element_type=jnp.float32)
+                    .astype(jnp.bfloat16)
+                    .reshape(n_dp, src_width, CAP_MOST, -1)
+                    for act in unit_acts
+                ],
+                axis=1,
+            )
+            for unit_acts, down in zip(acts, downs)
+        ]
+        return jnp.stack(outs, axis=1)
+
     weight_hi = weight.astype(jnp.bfloat16)
     weight_lo = (weight - weight_hi.astype(jnp.float32)).astype(jnp.bfloat16)
     halves_d = 2 if model_width % 256 == 0 else 1
@@ -241,7 +265,7 @@
     combined_parts = []
     for h in range(halves_d):
         cols = slice(h * piece_width, (h + 1) * piece_width)
-        y_recv = lax.all_to_all(y_send[..., cols], "dp", 0, 0, tiled=True)
+        y_recv = lax.all_to_all(returned_piece(cols), "dp", 0, 0, tiled=True)
         slot_out = [None] * slot_local
         for o in range(n_dp):
             for j, s in enumerate(owned_full[o]):

time: 408 us -> 390 us (0.956)
  waiting for transfers between devices: 208 us -> 177 us
  starting transfers between devices: 22.4 us -> 26.9 us
  local copies, waits for them, and re-layouts: 54.7 us -> 59.1 us
    ppermute x1, waiting for transfers between devices: 75.7 us -> 3.41 us  [on_device_body(): held.append(lax.ppermute(sent, 'dp', pairs))]
    all_to_all x3 -> x4, waiting for transfers between devices: 56.6 us -> 98.6 us  [the longest x2 52.1 us: on_device_body(): y_recv = lax.all_to_all(returned_piece(cols), 'dp', 0, 0, tiled=True)]
    all_to_all x3 -> x4, starting transfers between devices: 14.9 us -> 19.4 us  [the longest x2 9.71 us: on_device_body(): y_recv = lax.all_to_all(returned_piece(cols), 'dp', 0, 0, tiled=True)]
    unnamed x49 -> x62, local copies, waits for them, and re-layouts: 9.82 us -> 11.4 us
    dot_general x4 -> x12, matrix products: 8.03 us -> 9.34 us  [the longest x4 5.58 us: activate(): gate_up = jnp.dot(rows, w_up, preferred_element_type=jnp.float32)]
  transfers between devices with their start and end apart: 8 -> 9, of which waited for: 6 -> 8; matrix products, arithmetic and copies ran while one was open for 20% -> 24% of each run, Pallas kernels for 0% -> 0%
where the time goes in v3:
time: 390 us; the launch traced here: 388 us
  waiting for transfers between devices  177 us (45%)
  local copies, waits for them, and re-layouts  59.1 us (15%)
  blocking collectives  56.2 us (14%)
  other arithmetic  30.9 us (8%)
  starting transfers between devices  26.9 us (7%)
  matrix products  24 us (6%)
  between operations  14.6 us (4%)
    all_to_all x2, waiting for transfers between devices, on_device_body(): y_recv = lax.all_to_all(returned_piece(cols), 'dp', 0, 0, tiled=True)  52.1 us
    all_to_all x2, waiting for transfers between devices, on_device_body(): lax.all_to_all(x_send[:, :, p * src_width:(p + 1) * src_width], 'dp', 0,...  46.4 us
    all_to_all x1, blocking collectives, on_device_body(): lax.all_to_all(head_parts.reshape(n_dp, tok_rows, model_width), 'dp', 0,...  41.7 us
    all_to_all x1, waiting for transfers between devices, on_device_body(): weight_recv = lax.all_to_all(weight_send, 'dp', 0, 0, tiled=True)  39.2 us
    reduce_scatter x2, waiting for transfers between devices, on_device_body(): lax.psum_scatter(partial.reshape(n_exp * tok_rows, piece_width).astype(jn...  35.3 us
    all_gather x1, blocking collectives, on_device_body(): lax.all_gather(jnp.concatenate([expert_ids, replica_pick], axis=1), 'expe...  14.5 us
    another operation x16, local copies, waits for them, and re-layouts, as_rows(): return piece.reshape(-1, lane_width)  13 us
    unnamed x62, local copies, waits for them, and re-layouts  11.4 us
  transfers between devices with their start and end apart: 9, of which 8 were waited for; matrix products, arithmetic and copies ran while one was open for 24% of the time, Pallas kernels for 0%

profile of v3, /device:TPU:0, one launch (start us, length us, event | category | flops | bytes accessed | tf_op | source)
XLA Modules:
  0.0 388.2 jit_solution(6632817116521486769)
XLA Ops:
  10.4 41.7 %all_to_all.30 = f32[4,128,1536]{2,1,0:T(8,128)} all-to-all(f32[4,128,1536]{2,1,0:T(8,128)S(1)} %fusion.13), channel_id=1, replica_groups=mesh['dp'=4,'expert'=8] {'dp'}, dimensions={0} | all-to-all | bytes 6291456 | tf_op jit(solution)/shard_map/all_to_all | solution.py:171
  63.1 2.7 dynamic-slice_bitcast_fusion
  68.8 3.5 fusion.73
  76.5 4.6 %maximum_bitcast_fusion.2 = (bf16[1,1536,512]{2,1,0:T(8,128)(2,1)S(1)}, bf16[1,1536,512]{2,1,0:T(8,128)(2,1)S(1)}) fusion(bf16[192,512]{1,0:T(8,128)(2,1)} %reshape_squeeze.72, bf16[192,512]{1,0:T(8,128)(2,1)} %reshape_squeeze.71, bf16[384,512]{1,0:T(8,128)(2,1)} %reshape_squeeze.70, bf16[768,512]{1,0:T(8,128)(2,1)} %reshape_squeeze.69, ...), kind=kLoop, calls=%fused_computation.25 | loop fusion | flops 12582912 | bytes 6291456 | tf_op jit(solution)/shard_map/stack | solution.py:124
  81.4 3.2 pad_maximum_fusion.1
  84.6 5.4 %all-to-all-start.2 = ((bf16[4,1536,512]{2,1,0:T(8,128)(2,1)}), bf16[4,1536,512]{2,1,0:T(8,128)(2,1)}, u32[]{:S(2)}, u32[]{:S(2)}) async-start(bf16[4,1536,512]{2,1,0:T(8,128)(2,1)} %pad_maximum_fusion.1), calls=%async_computation.2 | async-start | bytes 12582912 | tf_op jit(solution)/shard_map/all_to_all | solution.py:125
  90.0 14.5 %all_gather.6 = s32[1024,16]{0,1:T(8,128)S(1)} all-gather(s32[128,16]{0,1:T(8,128)S(1)} %pad_add_fusion), channel_id=1, replica_groups=mesh['dp'=4,'expert'=8] {'expert'}, dimensions={0}, use_global_device_ids=true | all-gather | bytes 73728 | tf_op jit(solution)/shard_map/all_gather | solution.py:165
  111.2 3.3 convolution_convert_fusion
  116.4 3.0 fusion.71
  119.4 39.2 %all-to-all-done.2 = bf16[4,1536,512]{2,1,0:T(8,128)(2,1)} async-done(((bf16[4,1536,512]{2,1,0:T(8,128)(2,1)}), bf16[4,1536,512]{2,1,0:T(8,128)(2,1)}, u32[]{:S(2)}, u32[]{:S(2)}) %all-to-all-start.2) | async-done | bytes 6291488 | tf_op jit(solution)/shard_map/all_to_all | solution.py:125
  158.6 4.8 %all-to-all-start.1 = ((bf16[4,2,4,32,1536]{4,3,2,1,0:T(8,128)(2,1)}), bf16[4,2,4,32,1536]{4,3,2,1,0:T(8,128)(2,1)}, u32[]{:S(2)}, u32[]{:S(2)}) async-start(bf16[4,2,4,32,1536]{4,3,2,1,0:T(8,128)(2,1)} %get-tuple-element.8), calls=%async_computation.1 | async-start | bytes 6291456 | tf_op jit(solution)/shard_map/all_to_all | solution.py:213
  165.4 35.6 %all-to-all-done.1 = bf16[4,2,4,32,1536]{4,3,2,1,0:T(8,128)(2,1)} async-done(((bf16[4,2,4,32,1536]{4,3,2,1,0:T(8,128)(2,1)}), bf16[4,2,4,32,1536]{4,3,2,1,0:T(8,128)(2,1)}, u32[]{:S(2)}, u32[]{:S(2)}) %all-to-all-start.1) | async-done | bytes 3145760 | tf_op jit(solution)/shard_map/all_to_all | solution.py:213
  201.0 4.9 %all-to-all-start.3 = ((bf16[4,2,4,32,1536]{4,3,2,1,0:T(8,128)(2,1)}), bf16[4,2,4,32,1536]{4,3,2,1,0:T(8,128)(2,1)}, u32[]{:S(2)}, u32[]{:S(2)}) async-start(bf16[4,2,4,32,1536]{4,3,2,1,0:T(8,128)(2,1)} %get-tuple-element.9), calls=%async_computation.3 | async-start | bytes 6291456 | tf_op jit(solution)/shard_map/all_to_all | solution.py:213
  205.9 3.4 collective-permute-done
  213.0 3.8 slice.264
  216.7 5.6 %reshape_reshape.6 = bf16[1536,1024]{1,0:T(8,128)(2,1)} reshape(bf16[4,768,512]{2,1,0:T(8,128)(2,1)} %slice.264) | data formatting | bytes 6291456 | tf_op jit(solution)/shard_map/reshape;reshape | solution.py:138
  226.6 2.7 fusion.75
  230.4 10.9 %all-to-all-done.3 = bf16[4,2,4,32,1536]{4,3,2,1,0:T(8,128)(2,1)} async-done(((bf16[4,2,4,32,1536]{4,3,2,1,0:T(8,128)(2,1)}), bf16[4,2,4,32,1536]{4,3,2,1,0:T(8,128)(2,1)}, u32[]{:S(2)}, u32[]{:S(2)}) %all-to-all-start.3) | async-done | bytes 3145760 | tf_op jit(solution)/shard_map/all_to_all | solution.py:213
  254.9 5.0 %all-to-all-start.5 = ((bf16[4,2,8,32,768]{4,3,2,1,0:T(8,128)(2,1)}), bf16[4,2,8,32,768]{4,3,2,1,0:T(8,128)(2,1)}, u32[]{:S(2)}, u32[]{:S(2)}) async-start(bf16[4,2,8,32,768]{4,3,2,1,0:T(8,128)(2,1)} %pad_maximum_fusion.3), calls=%async_computation.6 | async-start | bytes 6291456 | tf_op jit(solution)/shard_map/all_to_all | solution.py:268
  260.0 3.0 convolution_bitcast_fusion
  268.8 25.8 %all-to-all-done.5 = bf16[4,2,8,32,768]{4,3,2,1,0:T(8,128)(2,1)} async-done(((bf16[4,2,8,32,768]{4,3,2,1,0:T(8,128)(2,1)}), bf16[4,2,8,32,768]{4,3,2,1,0:T(8,128)(2,1)}, u32[]{:S(2)}, u32[]{:S(2)}) %all-to-all-start.5) | async-done | bytes 3145760 | tf_op jit(solution)/shard_map/all_to_all | solution.py:268
  294.6 4.7 %all-to-all-start.4 = ((bf16[4,2,8,32,768]{4,3,2,1,0:T(8,128)(2,1)}), bf16[4,2,8,32,768]{4,3,2,1,0:T(8,128)(2,1)}, u32[]{:S(2)}, u32[]{:S(2)}) async-start(bf16[4,2,8,32,768]{4,3,2,1,0:T(8,128)(2,1)} %pad_maximum_fusion.2), calls=%async_computation.4 | async-start | bytes 6291456 | tf_op jit(solution)/shard_map/all_to_all | solution.py:268
  308.6 26.4 %all-to-all-done.4 = bf16[4,2,8,32,768]{4,3,2,1,0:T(8,128)(2,1)} async-done(((bf16[4,2,8,32,768]{4,3,2,1,0:T(8,128)(2,1)}), bf16[4,2,8,32,768]{4,3,2,1,0:T(8,128)(2,1)}, u32[]{:S(2)}, u32[]{:S(2)}) %all-to-all-start.4) | async-done | bytes 3145760 | tf_op jit(solution)/shard_map/all_to_all | solution.py:268
  344.7 34.8 %reduce-scatter.3.cloned.1.call-done = bf16[128,768]{1,0:T(8,128)(2,1)} async-done(((bf16[1024,768]{1,0:T(8,128)(2,1)}), bf16[128,768]{1,0:T(8,128)(2,1)}) %reduce-scatter.3.cloned.1.call-update) | async-done | bytes 196624 | tf_op jit(solution)/shard_map/reduce_scatter | solution.py:284
  (166 shorter events, 81.3 us)
Async XLA Ops:
  7.2 104.0 %all-gather.2.cloned.1.call-start = ((), (), s32[]{:S(2)}) async-start(), calls=%async_computation.8 | async-start | bytes 3538944 | tf_op jit(solution)/shard_map/all_gather | solution.py:180
  76.4 4.7 %copy-start.5 = (bf16[384,512]{1,0:T(8,128)(2,1)S(1)}, bf16[384,512]{1,0:T(8,128)(2,1)}, u32[]{:S(2)}) copy-start(bf16[384,512]{1,0:T(8,128)(2,1)} %reshape_squeeze.62) | copy-start | bytes 1179652
  76.4 4.7 %copy-start.7 = (bf16[192,512]{1,0:T(8,128)(2,1)S(1)}, bf16[192,512]{1,0:T(8,128)(2,1)}, u32[]{:S(2)}) copy-start(bf16[192,512]{1,0:T(8,128)(2,1)} %reshape_squeeze.63) | copy-start | bytes 589828
  76.4 4.7 %copy-start.8 = (bf16[192,512]{1,0:T(8,128)(2,1)S(1)}, bf16[192,512]{1,0:T(8,128)(2,1)}, u32[]{:S(2)}) copy-start(bf16[192,512]{1,0:T(8,128)(2,1)} %reshape_squeeze.68) | copy-start | bytes 589828
  76.4 4.7 %copy-start.9 = (bf16[192,512]{1,0:T(8,128)(2,1)S(1)}, bf16[192,512]{1,0:T(8,128)(2,1)}, u32[]{:S(2)}) copy-start(bf16[192,512]{1,0:T(8,128)(2,1)} %reshape_squeeze.67) | copy-start | bytes 589828
  76.4 4.7 %copy-start.10 = (bf16[192,512]{1,0:T(8,128)(2,1)S(1)}, bf16[192,512]{1,0:T(8,128)(2,1)}, u32[]{:S(2)}) copy-start(bf16[192,512]{1,0:T(8,128)(2,1)} %reshape_squeeze.64) | copy-start | bytes 589828
  84.6 5.4 %copy-start.23 = (s32[128,8]{0,1:T(8,128)S(1)}, s32[128,8]{0,1:T(8,128)}, u32[]{:S(2)}) copy-start(s32[128,8]{0,1:T(8,128)} %param.19) | copy-start | bytes 12292
  84.6 5.4 %copy-start.24 = (s32[128,8]{0,1:T(8,128)S(1)}, s32[128,8]{0,1:T(8,128)}, u32[]{:S(2)}) copy-start(s32[128,8]{0,1:T(8,128)} %param.18) | copy-start | bytes 12292
  84.6 20.2 %copy-start.22 = (s32[48]{0:T(128)S(1)}, s32[48]{0:T(128)}, u32[]{:S(2)}) copy-start(s32[48]{0:T(128)} %param.20) | copy-start | bytes 580
  84.6 74.0 %all-to-all-start.2 = ((bf16[4,1536,512]{2,1,0:T(8,128)(2,1)}), bf16[4,1536,512]{2,1,0:T(8,128)(2,1)}, u32[]{:S(2)}, u32[]{:S(2)}) async-start(bf16[4,1536,512]{2,1,0:T(8,128)(2,1)} %pad_maximum_fusion.1), calls=%async_computation.2 | async-start | bytes 12582912 | tf_op jit(solution)/shard_map/all_to_all | solution.py:125
  158.6 4.8 %copy-start.15 = (bf16[128,1536]{1,0:T(8,128)(2,1)S(1)}, bf16[128,1536]{1,0:T(8,128)(2,1)}, u32[]{:S(2)}) copy-start(bf16[128,1536]{1,0:T(8,128)(2,1)} %get-tuple-element.34) | copy-start | bytes 1179652
  158.6 42.3 %all-to-all-start.1 = ((bf16[4,2,4,32,1536]{4,3,2,1,0:T(8,128)(2,1)}), bf16[4,2,4,32,1536]{4,3,2,1,0:T(8,128)(2,1)}, u32[]{:S(2)}, u32[]{:S(2)}) async-start(bf16[4,2,4,32,1536]{4,3,2,1,0:T(8,128)(2,1)} %get-tuple-element.8), calls=%async_computation.1 | async-start | bytes 6291456 | tf_op jit(solution)/shard_map/all_to_all | solution.py:213
  163.4 45.8 %collective-permute-start = (bf16[128,1536]{1,0:T(8,128)(2,1)S(1)}, bf16[128,1536]{1,0:T(8,128)(2,1)S(1)}, u32[]{:S(2)}, u32[]{:S(2)}) collective-permute-start(bf16[128,1536]{1,0:T(8,128)(2,1)S(1)} %copy-done.15), channel_id=1, source_target_pairs={{8,0},{0,8},{24,16},{16,24},{9,1},{1,9},{25,17},{17,25},{10,2},{2,... | collective-permute-start | bytes 1179656 | tf_op jit(solution)/shard_map/ppermute | solution.py:160
  201.0 40.3 %all-to-all-start.3 = ((bf16[4,2,4,32,1536]{4,3,2,1,0:T(8,128)(2,1)}), bf16[4,2,4,32,1536]{4,3,2,1,0:T(8,128)(2,1)}, u32[]{:S(2)}, u32[]{:S(2)}) async-start(bf16[4,2,4,32,1536]{4,3,2,1,0:T(8,128)(2,1)} %get-tuple-element.9), calls=%async_computation.3 | async-start | bytes 6291456 | tf_op jit(solution)/shard_map/all_to_all | solution.py:213
  226.6 2.7 copy-start.16
  254.9 5.1 %copy-start.19 = (bf16[1536,40]{0,1:T(8,128)(2,1)S(1)}, bf16[1536,40]{0,1:T(8,128)(2,1)}, u32[]{:S(2)}) copy-start(bf16[1536,40]{0,1:T(8,128)(2,1)} %param.17) | copy-start | bytes 368644
  254.9 39.6 %all-to-all-start.5 = ((bf16[4,2,8,32,768]{4,3,2,1,0:T(8,128)(2,1)}), bf16[4,2,8,32,768]{4,3,2,1,0:T(8,128)(2,1)}, u32[]{:S(2)}, u32[]{:S(2)}) async-start(bf16[4,2,8,32,768]{4,3,2,1,0:T(8,128)(2,1)} %pad_maximum_fusion.3), calls=%async_computation.6 | async-start | bytes 6291456 | tf_op jit(solution)/shard_map/all_to_all | solution.py:268
  260.0 4.5 %copy-start.4 = (bf16[512,1536]{1,0:T(8,128)(2,1)S(1)}, bf16[512,1536]{1,0:T(8,128)(2,1)}, u32[]{:S(2)}) copy-start(bf16[512,1536]{1,0:T(8,128)(2,1)} %reshape_reshape.7) | copy-start | bytes 4718596
  260.0 4.5 %copy-start.14 = (bf16[512,512]{1,0:T(8,128)(2,1)S(1)}, bf16[512,512]{1,0:T(8,128)(2,1)}, u32[]{:S(2)}) copy-start(bf16[512,512]{1,0:T(8,128)(2,1)} %copy-done.13) | copy-start | bytes 1572868
  294.6 40.3 %all-to-all-start.4 = ((bf16[4,2,8,32,768]{4,3,2,1,0:T(8,128)(2,1)}), bf16[4,2,8,32,768]{4,3,2,1,0:T(8,128)(2,1)}, u32[]{:S(2)}, u32[]{:S(2)}) async-start(bf16[4,2,8,32,768]{4,3,2,1,0:T(8,128)(2,1)} %pad_maximum_fusion.2), calls=%async_computation.4 | async-start | bytes 6291456 | tf_op jit(solution)/shard_map/all_to_all | solution.py:268
  299.2 45.5 %reduce-scatter.5.cloned.1.call-start = ((), (), s32[]{:S(2)}) async-start(), calls=%async_computation.10 | async-start | bytes 1769472 | tf_op jit(solution)/shard_map/reduce_scatter | solution.py:284
  308.5 71.0 %reduce-scatter.3.cloned.1.call-start = ((), (), s32[]{:S(2)}) async-start(), calls=%async_computation.9 | async-start | bytes 1769472 | tf_op jit(solution)/shard_map/reduce_scatter | solution.py:284
  342.3 39.3 %copy-start.1 = (bf16[384,1536]{1,0:T(8,128)(2,1)S(1)}, bf16[384,1536]{1,0:T(8,128)(2,1)}, u32[]{:S(2)}) copy-start(bf16[384,1536]{1,0:T(8,128)(2,1)} %param.13) | copy-start | bytes 3538948
  344.1 36.6 %copy-start.21 = (f32[1536]{0:T(1024)S(1)}, f32[1536]{0:T(1024)}, u32[]{:S(2)}) copy-start(f32[1536]{0:T(1024)} %param.16) | copy-start | bytes 18436
  (11 other events, 20.5 us)
Sparse Core Ops, SparseCore 0:
  55.6 37.9 all-gather.1
  308.6 36.0 reduce-scatter.4
  347.0 32.4 reduce-scatter.2

commit v4 on v2

--- a/solution.py
+++ b/solution.py
@@ -168,10 +168,21 @@
 
     flat_context = context.reshape(-1, context.shape[3])
     head_parts = jnp.dot(flat_context, w_proj, preferred_element_type=jnp.float32)
-    head_parts = lax.all_to_all(
-        head_parts.reshape(n_dp, tok_rows, model_width), "dp", 0, 0, tiled=True
-    )
-    attended = jnp.sum(head_parts, axis=0)
+    split_at = model_width // 2 if model_width % 256 == 0 else model_width
+    attended_lo = lax.psum_scatter(
+        head_parts[:, :split_at], "dp", scatter_dimension=0, tiled=True
+    )
+    parts = [attended_lo]
+    if split_at < model_width:
+        swapped = lax.all_to_all(
+            head_parts[:, split_at:].reshape(n_dp, tok_rows, model_width - split_at),
+            "dp",
+            0,
+            0,
+            tiled=True,
+        )
+        parts.append(jnp.sum(swapped, axis=0))
+    attended = jnp.concatenate(parts, axis=-1)
     hidden_state = (residual.astype(jnp.float32) + attended.astype(jnp.float32)).astype(
         jnp.bfloat16
     )
@@ -210,15 +221,15 @@
 
     unit_rows = n_dp * n_exp * CAP_MOST
 
-    def expert_rows(rows, w_up, w_down, width):
+    def activate(rows, w_up, width):
         gate_up = jnp.dot(rows, w_up, preferred_element_type=jnp.float32)
-        activated = (jax.nn.silu(gate_up[:, :width]) * gate_up[:, width:]).astype(jnp.bfloat16)
-        return jnp.dot(activated, w_down, preferred_element_type=jnp.float32).astype(jnp.bfloat16)
-
-    outs = []
+        return (jax.nn.silu(gate_up[:, :width]) * gate_up[:, width:]).astype(jnp.bfloat16)
+
+    acts, downs = [], []
     for j in range(full):
         rows = x_recv[:, j].reshape(unit_rows, model_width)
-        outs.append(expert_rows(rows, full_in[j], full_out[j], hidden_units))
+        acts.append(activate(rows, full_in[j], hidden_units))
+        downs.append(full_out[j])
     for i in range(halves):
         rows = x_recv[:, full + i].reshape(unit_rows, model_width)
         if paired:
@@ -228,12 +239,18 @@
             w_down = lax.dynamic_slice_in_dim(
                 part_out[i], chunk_at * sources_per_chunk, sources_per_chunk, axis=0
             ).reshape(chunk_width, model_width)
-        outs.append(expert_rows(rows, part_in[i], w_down, chunk_width))
-    y_send = (
-        jnp.stack(outs)
-        .reshape(full + halves, n_dp, n_exp, CAP_MOST, model_width)
-        .transpose(1, 0, 2, 3, 4)
-    )
+        acts.append(activate(rows, part_in[i], chunk_width))
+        downs.append(w_down)
+
+    def returned_piece(cols):
+        outs = [
+            jnp.dot(act, down[:, cols], preferred_element_type=jnp.float32)
+            .astype(jnp.bfloat16)
+            .reshape(n_dp, n_exp, CAP_MOST, -1)
+            for act, down in zip(acts, downs)
+        ]
+        return jnp.stack(outs, axis=1)
+
     weight_hi = weight.astype(jnp.bfloat16)
     weight_lo = (weight - weight_hi.astype(jnp.float32)).astype(jnp.bfloat16)
     halves_d = 2 if model_width % 256 == 0 else 1
@@ -241,7 +258,7 @@
     combined_parts = []
     for h in range(halves_d):
         cols = slice(h * piece_width, (h + 1) * piece_width)
-        y_recv = lax.all_to_all(y_send[..., cols], "dp", 0, 0, tiled=True)
+        y_recv = lax.all_to_all(returned_piece(cols), "dp", 0, 0, tiled=True)
         slot_out = [None] * slot_local
         for o in range(n_dp):
             for j, s in enumerate(owned_full[o]):

time: 408 us -> 414 us (1.015)
  waiting for transfers between devices: 208 us -> 219 us
  blocking collectives: 56.1 us -> 47.7 us
    reduce_scatter x0 -> x1, waiting for transfers between devices: none -> 13.6 us  [on_device_body(): lax.psum_scatter(head_parts[:, :split_at], 'dp', scatter_dimension=0, til...]
    all_to_all x1, blocking collectives: 41.7 us -> 33.5 us  [on_device_body(): lax.all_to_all(head_parts[:, split_at:].reshape(n_dp, tok_rows, model_wid...]
    unnamed x49 -> x55, local copies, waits for them, and re-layouts: 9.82 us -> 10.7 us
    dot_general x4 -> x6, matrix products: 8.03 us -> 8.29 us  [the longest x2 5.19 us: activate(): gate_up = jnp.dot(rows, w_up, preferred_element_type=jnp.float32)]
  transfers between devices with their start and end apart: 8 -> 9, of which waited for: 6 -> 7; matrix products, arithmetic and copies ran while one was open for 20% -> 21% of each run, Pallas kernels for 0% -> 0%
where the time goes in v4:
time: 414 us; the launch traced here: 413 us
  waiting for transfers between devices  219 us (53%)
  local copies, waits for them, and re-layouts  53.9 us (13%)
  blocking collectives  47.7 us (12%)
  other arithmetic  32.5 us (8%)
  matrix products  22.8 us (6%)
  starting transfers between devices  22.4 us (5%)
  between operations  14.5 us (4%)
    ppermute x1, waiting for transfers between devices, on_device_body(): held.append(lax.ppermute(sent, 'dp', pairs))  75.7 us
    all_to_all x2, waiting for transfers between devices, on_device_body(): y_recv = lax.all_to_all(returned_piece(cols), 'dp', 0, 0, tiled=True)  53.3 us
    all_to_all x1, waiting for transfers between devices, on_device_body(): weight_recv = lax.all_to_all(weight_send, 'dp', 0, 0, tiled=True)  41.2 us
    reduce_scatter x2, waiting for transfers between devices, on_device_body(): lax.psum_scatter(partial.reshape(n_exp * tok_rows, piece_width).astype(jn...  34.9 us
    all_to_all x1, blocking collectives, on_device_body(): lax.all_to_all(head_parts[:, split_at:].reshape(n_dp, tok_rows, model_wid...  33.5 us
    all_gather x1, blocking collectives, on_device_body(): lax.all_gather(jnp.concatenate([expert_ids, replica_pick], axis=1), 'expe...  14.2 us
    reduce_scatter x1, waiting for transfers between devices, on_device_body(): lax.psum_scatter(head_parts[:, :split_at], 'dp', scatter_dimension=0, til...  13.6 us
    another operation x16, local copies, waits for them, and re-layouts, as_rows(): return piece.reshape(-1, lane_width)  13.1 us
  transfers between devices with their start and end apart: 9, of which 7 were waited for; matrix products, arithmetic and copies ran while one was open for 21% of the time, Pallas kernels for 0%

profile of v4, /device:TPU:0, one launch (start us, length us, event | category | flops | bytes accessed | tf_op | source)
XLA Modules:
  0.0 412.7 jit_solution(17320725310187876430)
XLA Ops:
  12.4 33.5 %all_to_all.25 = f32[4,128,768]{2,1,0:T(8,128)S(1)} all-to-all(f32[4,128,768]{2,1,0:T(8,128)} %bitcast.153), channel_id=1, replica_groups=mesh['dp'=4,'expert'=8] {'dp'}, dimensions={0} | all-to-all | bytes 3145728 | tf_op jit(solution)/shard_map/all_to_all | solution.py:177
  46.0 13.6 %reduce-scatter.4.cloned.1.call-done = f32[128,768]{1,0:T(8,128)} async-done(((f32[512,768]{1,0:T(8,128)}), f32[128,768]{1,0:T(8,128)}) %reduce-scatter.4.cloned.1.call-update) | async-done | bytes 393232 | tf_op jit(solution)/shard_map/reduce_scatter | solution.py:172
  69.3 2.8 dynamic-slice_bitcast_fusion
  75.1 3.5 fusion.71
  82.8 4.6 %maximum_bitcast_fusion.2 = (bf16[1,1536,512]{2,1,0:T(8,128)(2,1)S(1)}, bf16[1,1536,512]{2,1,0:T(8,128)(2,1)S(1)}) fusion(bf16[192,512]{1,0:T(8,128)(2,1)} %reshape_squeeze.66, bf16[192,512]{1,0:T(8,128)(2,1)} %reshape_squeeze.65, bf16[384,512]{1,0:T(8,128)(2,1)} %reshape_squeeze.64, bf16[768,512]{1,0:T(8,128)(2,1)} %reshape_squeeze.63, ...), kind=kLoop, calls=%fused_computation.31 | loop fusion | flops 12582912 | bytes 6291456 | tf_op jit(solution)/shard_map/stack | solution.py:124
  87.7 3.1 pad_maximum_fusion.1
  90.8 5.4 %all-to-all-start.2 = ((bf16[4,1536,512]{2,1,0:T(8,128)(2,1)}), bf16[4,1536,512]{2,1,0:T(8,128)(2,1)}, u32[]{:S(2)}, u32[]{:S(2)}) async-start(bf16[4,1536,512]{2,1,0:T(8,128)(2,1)} %pad_maximum_fusion.1), calls=%async_computation.3 | async-start | bytes 12582912 | tf_op jit(solution)/shard_map/all_to_all | solution.py:125
  96.3 14.2 %all_gather.6 = s32[1024,16]{0,1:T(8,128)S(1)} all-gather(s32[128,16]{0,1:T(8,128)S(1)} %pad_add_fusion), channel_id=1, replica_groups=mesh['dp'=4,'expert'=8] {'expert'}, dimensions={0}, use_global_device_ids=true | all-gather | bytes 73728 | tf_op jit(solution)/shard_map/all_gather | solution.py:165
  117.1 3.3 convolution_convert_fusion
  121.5 3.4 pad_maximum_fusion
  124.8 41.2 %all-to-all-done.2 = bf16[4,1536,512]{2,1,0:T(8,128)(2,1)} async-done(((bf16[4,1536,512]{2,1,0:T(8,128)(2,1)}), bf16[4,1536,512]{2,1,0:T(8,128)(2,1)}, u32[]{:S(2)}, u32[]{:S(2)}) %all-to-all-start.2) | async-done | bytes 6291488 | tf_op jit(solution)/shard_map/all_to_all | solution.py:125
  166.0 5.5 %all-to-all-start.1 = ((bf16[4,2,8,32,1536]{4,3,2,1,0:T(8,128)(2,1)}), bf16[4,2,8,32,1536]{4,3,2,1,0:T(8,128)(2,1)}, u32[]{:S(2)}, u32[]{:S(2)}) async-start(bf16[4,2,8,32,1536]{4,3,2,1,0:T(8,128)(2,1)} %pad_maximum_fusion), calls=%async_computation.2 | async-start | bytes 12582912 | tf_op jit(solution)/shard_map/all_to_all | solution.py:220
  173.3 75.7 %collective-permute-done = bf16[128,1536]{1,0:T(8,128)(2,1)S(1)} collective-permute-done((bf16[128,1536]{1,0:T(8,128)(2,1)S(1)}, bf16[128,1536]{1,0:T(8,128)(2,1)S(1)}, u32[]{:S(2)}, u32[]{:S(2)}) %collective-permute-start) | collective-permute-done | bytes 393248 | tf_op jit(solution)/shard_map/ppermute | solution.py:160
  253.6 3.8 slice.237
  257.5 5.7 %reshape_reshape.6 = bf16[1536,1024]{1,0:T(8,128)(2,1)} reshape(bf16[4,768,512]{2,1,0:T(8,128)(2,1)} %slice.237) | data formatting | bytes 6291456 | tf_op jit(solution)/shard_map/reshape;reshape | solution.py:138
  265.2 3.4 fusion.69
  269.0 3.4 fusion.76
  279.6 4.8 %all-to-all-start.4 = ((bf16[4,2,8,32,768]{4,3,2,1,0:T(8,128)(2,1)}), bf16[4,2,8,32,768]{4,3,2,1,0:T(8,128)(2,1)}, u32[]{:S(2)}, u32[]{:S(2)}) async-start(bf16[4,2,8,32,768]{4,3,2,1,0:T(8,128)(2,1)} %pad_maximum_fusion.3), calls=%async_computation.6 | async-start | bytes 6291456 | tf_op jit(solution)/shard_map/all_to_all | solution.py:261
  284.3 2.9 convolution_bitcast_fusion
  290.3 2.0 pad_maximum_fusion.2
  292.3 26.9 %all-to-all-done.4 = bf16[4,2,8,32,768]{4,3,2,1,0:T(8,128)(2,1)} async-done(((bf16[4,2,8,32,768]{4,3,2,1,0:T(8,128)(2,1)}), bf16[4,2,8,32,768]{4,3,2,1,0:T(8,128)(2,1)}, u32[]{:S(2)}, u32[]{:S(2)}) %all-to-all-start.4) | async-done | bytes 3145760 | tf_op jit(solution)/shard_map/all_to_all | solution.py:261
  319.2 4.9 %all-to-all-start.3 = ((bf16[4,2,8,32,768]{4,3,2,1,0:T(8,128)(2,1)}), bf16[4,2,8,32,768]{4,3,2,1,0:T(8,128)(2,1)}, u32[]{:S(2)}, u32[]{:S(2)}) async-start(bf16[4,2,8,32,768]{4,3,2,1,0:T(8,128)(2,1)} %pad_maximum_fusion.2), calls=%async_computation.4 | async-start | bytes 6291456 | tf_op jit(solution)/shard_map/all_to_all | solution.py:261
  333.4 26.4 %all-to-all-done.3 = bf16[4,2,8,32,768]{4,3,2,1,0:T(8,128)(2,1)} async-done(((bf16[4,2,8,32,768]{4,3,2,1,0:T(8,128)(2,1)}), bf16[4,2,8,32,768]{4,3,2,1,0:T(8,128)(2,1)}, u32[]{:S(2)}, u32[]{:S(2)}) %all-to-all-start.3) | async-done | bytes 3145760 | tf_op jit(solution)/shard_map/all_to_all | solution.py:261
  369.3 34.6 %reduce-scatter.6.cloned.1.call-done = bf16[128,768]{1,0:T(8,128)(2,1)} async-done(((bf16[1024,768]{1,0:T(8,128)(2,1)}), bf16[128,768]{1,0:T(8,128)(2,1)}) %reduce-scatter.6.cloned.1.call-update) | async-done | bytes 196624 | tf_op jit(solution)/shard_map/reduce_scatter | solution.py:277
  (146 shorter events, 69.7 us)
Async XLA Ops:
  7.2 52.4 %reduce-scatter.4.cloned.1.call-start = ((), (), s32[]{:S(2)}) async-start(), calls=%async_computation.8 | async-start | bytes 1966080 | tf_op jit(solution)/shard_map/reduce_scatter | solution.py:172
  12.3 104.8 %all-gather.2.cloned.1.call-start = ((), (), s32[]{:S(2)}) async-start(), calls=%async_computation.9 | async-start | bytes 3538944 | tf_op jit(solution)/shard_map/all_gather | solution.py:191
  12.4 47.3 %copy-start.15 = (bf16[128,1536]{1,0:T(8,128)(2,1)S(1)}, bf16[128,1536]{1,0:T(8,128)(2,1)}, u32[]{:S(2)}) copy-start(bf16[128,1536]{1,0:T(8,128)(2,1)} %param.14) | copy-start | bytes 1179652
  45.9 14.9 %copy-start.17 = (f32[1536]{0:T(1024)S(1)}, f32[1536]{0:T(1024)}, u32[]{:S(2)}) copy-start(f32[1536]{0:T(1024)} %param.15) | copy-start | bytes 18436
  82.7 4.7 %copy-start.6 = (bf16[384,512]{1,0:T(8,128)(2,1)S(1)}, bf16[384,512]{1,0:T(8,128)(2,1)}, u32[]{:S(2)}) copy-start(bf16[384,512]{1,0:T(8,128)(2,1)} %reshape_squeeze.56) | copy-start | bytes 1179652
  82.7 4.7 %copy-start.10 = (bf16[192,512]{1,0:T(8,128)(2,1)S(1)}, bf16[192,512]{1,0:T(8,128)(2,1)}, u32[]{:S(2)}) copy-start(bf16[192,512]{1,0:T(8,128)(2,1)} %reshape_squeeze.57) | copy-start | bytes 589828
  82.8 4.7 %copy-start.11 = (bf16[192,512]{1,0:T(8,128)(2,1)S(1)}, bf16[192,512]{1,0:T(8,128)(2,1)}, u32[]{:S(2)}) copy-start(bf16[192,512]{1,0:T(8,128)(2,1)} %reshape_squeeze.62) | copy-start | bytes 589828
  82.8 4.7 %copy-start.12 = (bf16[192,512]{1,0:T(8,128)(2,1)S(1)}, bf16[192,512]{1,0:T(8,128)(2,1)}, u32[]{:S(2)}) copy-start(bf16[192,512]{1,0:T(8,128)(2,1)} %reshape_squeeze.61) | copy-start | bytes 589828
  82.8 4.7 %copy-start.13 = (bf16[192,512]{1,0:T(8,128)(2,1)S(1)}, bf16[192,512]{1,0:T(8,128)(2,1)}, u32[]{:S(2)}) copy-start(bf16[192,512]{1,0:T(8,128)(2,1)} %reshape_squeeze.58) | copy-start | bytes 589828
  90.8 5.4 %copy-start.20 = (s32[128,8]{0,1:T(8,128)S(1)}, s32[128,8]{0,1:T(8,128)}, u32[]{:S(2)}) copy-start(s32[128,8]{0,1:T(8,128)} %param.19) | copy-start | bytes 12292
  90.8 5.4 %copy-start.21 = (s32[128,8]{0,1:T(8,128)S(1)}, s32[128,8]{0,1:T(8,128)}, u32[]{:S(2)}) copy-start(s32[128,8]{0,1:T(8,128)} %param.18) | copy-start | bytes 12292
  90.8 19.9 %copy-start.19 = (s32[48]{0:T(128)S(1)}, s32[48]{0:T(128)}, u32[]{:S(2)}) copy-start(s32[48]{0:T(128)} %param.20) | copy-start | bytes 580
  90.8 75.2 %all-to-all-start.2 = ((bf16[4,1536,512]{2,1,0:T(8,128)(2,1)}), bf16[4,1536,512]{2,1,0:T(8,128)(2,1)}, u32[]{:S(2)}, u32[]{:S(2)}) async-start(bf16[4,1536,512]{2,1,0:T(8,128)(2,1)} %pad_maximum_fusion.1), calls=%async_computation.3 | async-start | bytes 12582912 | tf_op jit(solution)/shard_map/all_to_all | solution.py:125
  124.8 46.7 %copy-start.14 = (bf16[128,1536]{1,0:T(8,128)(2,1)S(1)}, bf16[128,1536]{1,0:T(8,128)(2,1)}, u32[]{:S(2)}) copy-start(bf16[128,1536]{1,0:T(8,128)(2,1)} %get-tuple-element.32) | copy-start | bytes 1179652
  166.0 99.2 %all-to-all-start.1 = ((bf16[4,2,8,32,1536]{4,3,2,1,0:T(8,128)(2,1)}), bf16[4,2,8,32,1536]{4,3,2,1,0:T(8,128)(2,1)}, u32[]{:S(2)}, u32[]{:S(2)}) async-start(bf16[4,2,8,32,1536]{4,3,2,1,0:T(8,128)(2,1)} %pad_maximum_fusion), calls=%async_computation.2 | async-start | bytes 12582912 | tf_op jit(solution)/shard_map/all_to_all | solution.py:220
  171.5 77.5 %collective-permute-start = (bf16[128,1536]{1,0:T(8,128)(2,1)S(1)}, bf16[128,1536]{1,0:T(8,128)(2,1)S(1)}, u32[]{:S(2)}, u32[]{:S(2)}) collective-permute-start(bf16[128,1536]{1,0:T(8,128)(2,1)S(1)} %copy-done.14), channel_id=1, source_target_pairs={{8,0},{0,8},{24,16},{16,24},{9,1},{1,9},{25,17},{17,25},{10,2},{2,... | collective-permute-start | bytes 1179656 | tf_op jit(solution)/shard_map/ppermute | solution.py:160
  265.2 3.7 copy-start.3
  279.6 4.8 %copy-start.16 = (bf16[1536,40]{0,1:T(8,128)(2,1)S(1)}, bf16[1536,40]{0,1:T(8,128)(2,1)}, u32[]{:S(2)}) copy-start(bf16[1536,40]{0,1:T(8,128)(2,1)} %param.17) | copy-start | bytes 368644
  279.6 39.6 %all-to-all-start.4 = ((bf16[4,2,8,32,768]{4,3,2,1,0:T(8,128)(2,1)}), bf16[4,2,8,32,768]{4,3,2,1,0:T(8,128)(2,1)}, u32[]{:S(2)}, u32[]{:S(2)}) async-start(bf16[4,2,8,32,768]{4,3,2,1,0:T(8,128)(2,1)} %pad_maximum_fusion.3), calls=%async_computation.6 | async-start | bytes 6291456 | tf_op jit(solution)/shard_map/all_to_all | solution.py:261
  319.2 40.6 %all-to-all-start.3 = ((bf16[4,2,8,32,768]{4,3,2,1,0:T(8,128)(2,1)}), bf16[4,2,8,32,768]{4,3,2,1,0:T(8,128)(2,1)}, u32[]{:S(2)}, u32[]{:S(2)}) async-start(bf16[4,2,8,32,768]{4,3,2,1,0:T(8,128)(2,1)} %pad_maximum_fusion.2), calls=%async_computation.4 | async-start | bytes 6291456 | tf_op jit(solution)/shard_map/all_to_all | solution.py:261
  324.1 45.2 %reduce-scatter.8.cloned.1.call-start = ((), (), s32[]{:S(2)}) async-start(), calls=%async_computation.11 | async-start | bytes 1769472 | tf_op jit(solution)/shard_map/reduce_scatter | solution.py:277
  333.4 70.6 %reduce-scatter.6.cloned.1.call-start = ((), (), s32[]{:S(2)}) async-start(), calls=%async_computation.10 | async-start | bytes 1769472 | tf_op jit(solution)/shard_map/reduce_scatter | solution.py:277
  367.2 38.9 %copy-start.1 = (bf16[384,1536]{1,0:T(8,128)(2,1)S(1)}, bf16[384,1536]{1,0:T(8,128)(2,1)}, u32[]{:S(2)}) copy-start(bf16[384,1536]{1,0:T(8,128)(2,1)} %param.13) | copy-start | bytes 3538948
  369.0 36.2 %copy-start.18 = (f32[1536]{0:T(1024)S(1)}, f32[1536]{0:T(1024)}, u32[]{:S(2)}) copy-start(f32[1536]{0:T(1024)} %param.16) | copy-start | bytes 18436
  (8 other events, 15.3 us)
Sparse Core Ops, SparseCore 0:
  12.4 47.1 reduce-scatter.3
  61.9 38.1 all-gather.1
  333.5 35.8 reduce-scatter.7
  371.5 32.3 reduce-scatter.5

commit v5 on v4

--- a/solution.py
+++ b/solution.py
@@ -168,21 +168,10 @@
 
     flat_context = context.reshape(-1, context.shape[3])
     head_parts = jnp.dot(flat_context, w_proj, preferred_element_type=jnp.float32)
-    split_at = model_width // 2 if model_width % 256 == 0 else model_width
-    attended_lo = lax.psum_scatter(
-        head_parts[:, :split_at], "dp", scatter_dimension=0, tiled=True
-    )
-    parts = [attended_lo]
-    if split_at < model_width:
-        swapped = lax.all_to_all(
-            head_parts[:, split_at:].reshape(n_dp, tok_rows, model_width - split_at),
-            "dp",
-            0,
-            0,
-            tiled=True,
-        )
-        parts.append(jnp.sum(swapped, axis=0))
-    attended = jnp.concatenate(parts, axis=-1)
+    head_parts = lax.all_to_all(
+        head_parts.reshape(n_dp, tok_rows, model_width), "dp", 0, 0, tiled=True
+    )
+    attended = jnp.sum(head_parts, axis=0)
     hidden_state = (residual.astype(jnp.float32) + attended.astype(jnp.float32)).astype(
         jnp.bfloat16
     )
@@ -253,7 +242,7 @@
 
     weight_hi = weight.astype(jnp.bfloat16)
     weight_lo = (weight - weight_hi.astype(jnp.float32)).astype(jnp.bfloat16)
-    halves_d = 2 if model_width % 256 == 0 else 1
+    halves_d = 1
     piece_width = model_width // halves_d
     combined_parts = []
     for h in range(halves_d):

time: 414 us -> 410 us (level)
  blocking collectives: 47.7 us -> 56.1 us
  local copies, waits for them, and re-layouts: 53.9 us -> 47.8 us
    reduce_scatter x1 -> x0, waiting for transfers between devices: 13.6 us -> none  [on_device_body(): lax.psum_scatter(head_parts[:, :split_at], 'dp', scatter_dimension=0, til...]
    all_to_all x2 -> x1, waiting for transfers between devices: 53.3 us -> 63.9 us  [on_device_body(): y_recv = lax.all_to_all(returned_piece(cols), 'dp', 0, 0, tiled=True)]
    all_to_all x1, blocking collectives: 33.5 us -> 41.7 us  [on_device_body(): lax.all_to_all(head_parts.reshape(n_dp, tok_rows, model_width), 'dp', 0,...]
    reduce_scatter x2 -> x1, waiting for transfers between devices: 34.9 us -> 40.7 us  [on_device_body(): lax.psum_scatter(partial.reshape(n_exp * tok_rows, piece_width).astype(jn...]
    unnamed x55 -> x45, local copies, waits for them, and re-layouts: 10.7 us -> 6.36 us
    all_to_all x2 -> x1, starting transfers between devices: 9.67 us -> 5.37 us  [on_device_body(): y_recv = lax.all_to_all(returned_piece(cols), 'dp', 0, 0, tiled=True)]
  transfers between devices with their start and end apart: 9 -> 6, of which waited for: 7 -> 4; matrix products, arithmetic and copies ran while one was open for 21% -> 16% of each run, Pallas kernels for 0% -> 0%
where the time goes in v5:
time: 410 us; the launch traced here: 409 us
  waiting for transfers between devices  220 us (54%)
  blocking collectives  56.1 us (14%)
  local copies, waits for them, and re-layouts  47.8 us (12%)
  other arithmetic  30.3 us (7%)
  matrix products  21.4 us (5%)
  starting transfers between devices  18.3 us (4%)
  between operations  14.6 us (4%)
    ppermute x1, waiting for transfers between devices, on_device_body(): held.append(lax.ppermute(sent, 'dp', pairs))  75.7 us
    all_to_all x1, waiting for transfers between devices, on_device_body(): y_recv = lax.all_to_all(returned_piece(cols), 'dp', 0, 0, tiled=True)  63.9 us
    all_to_all x1, blocking collectives, on_device_body(): lax.all_to_all(head_parts.reshape(n_dp, tok_rows, model_width), 'dp', 0,...  41.7 us
    reduce_scatter x1, waiting for transfers between devices, on_device_body(): lax.psum_scatter(partial.reshape(n_exp * tok_rows, piece_width).astype(jn...  40.7 us
    all_to_all x1, waiting for transfers between devices, on_device_body(): weight_recv = lax.all_to_all(weight_send, 'dp', 0, 0, tiled=True)  39.7 us
    all_gather x1, blocking collectives, on_device_body(): lax.all_gather(jnp.concatenate([expert_ids, replica_pick], axis=1), 'expe...  14.4 us
    another operation x16, local copies, waits for them, and re-layouts, as_rows(): return piece.reshape(-1, lane_width)  13.1 us
  transfers between devices with their start and end apart: 6, of which 4 were waited for; matrix products, arithmetic and copies ran while one was open for 16% of the time, Pallas kernels for 0%

profile of v5, /device:TPU:0, one launch (start us, length us, event | category | flops | bytes accessed | tf_op | source)
XLA Modules:
  0.0 408.8 jit_solution(14869611477328071467)
XLA Ops:
  8.4 2.0 fusion.18
  10.4 41.7 %all_to_all.20 = f32[4,128,1536]{2,1,0:T(8,128)} all-to-all(f32[4,128,1536]{2,1,0:T(8,128)S(1)} %fusion.18), channel_id=1, replica_groups=mesh['dp'=4,'expert'=8] {'dp'}, dimensions={0} | all-to-all | bytes 6291456 | tf_op jit(solution)/shard_map/all_to_all | solution.py:171
  52.1 2.2 reduce_sum.108
  63.1 2.7 fusion.67
  68.8 3.5 fusion.65
  76.5 4.6 %maximum_bitcast_fusion.2 = (bf16[1,1536,512]{2,1,0:T(8,128)(2,1)S(1)}, bf16[1,1536,512]{2,1,0:T(8,128)(2,1)S(1)}) fusion(bf16[192,512]{1,0:T(8,128)(2,1)} %reshape_squeeze.66, bf16[192,512]{1,0:T(8,128)(2,1)} %reshape_squeeze.65, bf16[384,512]{1,0:T(8,128)(2,1)} %reshape_squeeze.64, bf16[768,512]{1,0:T(8,128)(2,1)} %reshape_squeeze.63, ...), kind=kLoop, calls=%fused_computation.27 | loop fusion | flops 12582912 | bytes 6291456 | tf_op jit(solution)/shard_map/stack | solution.py:124
  81.4 3.2 pad_maximum_fusion.1
  84.6 5.4 %all-to-all-start.2 = ((bf16[4,1536,512]{2,1,0:T(8,128)(2,1)}), bf16[4,1536,512]{2,1,0:T(8,128)(2,1)}, u32[]{:S(2)}, u32[]{:S(2)}) async-start(bf16[4,1536,512]{2,1,0:T(8,128)(2,1)} %pad_maximum_fusion.1), calls=%async_computation.2 | async-start | bytes 12582912 | tf_op jit(solution)/shard_map/all_to_all | solution.py:125
  90.0 14.4 %all_gather.6 = s32[1024,16]{0,1:T(8,128)S(1)} all-gather(s32[128,16]{0,1:T(8,128)S(1)} %pad_add_fusion), channel_id=1, replica_groups=mesh['dp'=4,'expert'=8] {'expert'}, dimensions={0}, use_global_device_ids=true | all-gather | bytes 73728 | tf_op jit(solution)/shard_map/all_gather | solution.py:165
  111.2 3.3 convolution_convert_fusion
  115.5 3.4 pad_maximum_fusion
  118.8 39.7 %all-to-all-done.2 = bf16[4,1536,512]{2,1,0:T(8,128)(2,1)} async-done(((bf16[4,1536,512]{2,1,0:T(8,128)(2,1)}), bf16[4,1536,512]{2,1,0:T(8,128)(2,1)}, u32[]{:S(2)}, u32[]{:S(2)}) %all-to-all-start.2) | async-done | bytes 6291488 | tf_op jit(solution)/shard_map/all_to_all | solution.py:125
  158.6 5.5 %all-to-all-start.1 = ((bf16[4,2,8,32,1536]{4,3,2,1,0:T(8,128)(2,1)}), bf16[4,2,8,32,1536]{4,3,2,1,0:T(8,128)(2,1)}, u32[]{:S(2)}, u32[]{:S(2)}) async-start(bf16[4,2,8,32,1536]{4,3,2,1,0:T(8,128)(2,1)} %pad_maximum_fusion), calls=%async_computation.1 | async-start | bytes 12582912 | tf_op jit(solution)/shard_map/all_to_all | solution.py:209
  165.8 75.7 %collective-permute-done = bf16[128,1536]{1,0:T(8,128)(2,1)S(1)} collective-permute-done((bf16[128,1536]{1,0:T(8,128)(2,1)S(1)}, bf16[128,1536]{1,0:T(8,128)(2,1)S(1)}, u32[]{:S(2)}, u32[]{:S(2)}) %collective-permute-start) | collective-permute-done | bytes 393248 | tf_op jit(solution)/shard_map/ppermute | solution.py:160
  246.2 3.8 slice.179
  250.1 5.7 %reshape_reshape.6 = bf16[1536,1024]{1,0:T(8,128)(2,1)} reshape(bf16[4,768,512]{2,1,0:T(8,128)(2,1)} %slice.179) | data formatting | bytes 6291456 | tf_op jit(solution)/shard_map/reshape;reshape | solution.py:138
  257.8 3.4 fusion.63
  261.5 3.4 fusion.69
  269.6 3.2 pad_maximum_fusion.2
  272.8 5.4 %all-to-all-start.3 = ((bf16[4,2,8,32,1536]{4,3,2,1,0:T(8,128)(2,1)}), bf16[4,2,8,32,1536]{4,3,2,1,0:T(8,128)(2,1)}, u32[]{:S(2)}, u32[]{:S(2)}) async-start(bf16[4,2,8,32,1536]{4,3,2,1,0:T(8,128)(2,1)} %pad_maximum_fusion.2), calls=%async_computation.3 | async-start | bytes 12582912 | tf_op jit(solution)/shard_map/all_to_all | solution.py:250
  278.5 2.9 convolution_bitcast_fusion
  282.9 63.9 %all-to-all-done.3 = bf16[4,2,8,32,1536]{4,3,2,1,0:T(8,128)(2,1)} async-done(((bf16[4,2,8,32,1536]{4,3,2,1,0:T(8,128)(2,1)}), bf16[4,2,8,32,1536]{4,3,2,1,0:T(8,128)(2,1)}, u32[]{:S(2)}, u32[]{:S(2)}) %all-to-all-start.3) | async-done | bytes 6291488 | tf_op jit(solution)/shard_map/all_to_all | solution.py:250
  356.3 2.7 add_convert_fusion
  359.1 40.7 %reduce-scatter.2.cloned.1.call-done = bf16[128,1536]{1,0:T(8,128)(2,1)} async-done(((bf16[1024,1536]{1,0:T(8,128)(2,1)}), bf16[128,1536]{1,0:T(8,128)(2,1)}) %reduce-scatter.2.cloned.1.call-update) | async-done | bytes 393232 | tf_op jit(solution)/shard_map/reduce_scatter | solution.py:266
  (117 shorter events, 51.7 us)
Async XLA Ops:
  7.2 104.0 %all-gather.2.cloned.1.call-start = ((), (), s32[]{:S(2)}) async-start(), calls=%async_computation.5 | async-start | bytes 3538944 | tf_op jit(solution)/shard_map/all_gather | solution.py:180
  52.1 2.2 copy-start.12
  52.1 2.5 copy-start.14
  76.4 4.7 %copy-start.4 = (bf16[384,512]{1,0:T(8,128)(2,1)S(1)}, bf16[384,512]{1,0:T(8,128)(2,1)}, u32[]{:S(2)}) copy-start(bf16[384,512]{1,0:T(8,128)(2,1)} %reshape_squeeze.60) | copy-start | bytes 1179652
  76.5 4.7 %copy-start.6 = (bf16[192,512]{1,0:T(8,128)(2,1)S(1)}, bf16[192,512]{1,0:T(8,128)(2,1)}, u32[]{:S(2)}) copy-start(bf16[192,512]{1,0:T(8,128)(2,1)} %reshape_squeeze.57) | copy-start | bytes 589828
  76.5 4.7 %copy-start.7 = (bf16[192,512]{1,0:T(8,128)(2,1)S(1)}, bf16[192,512]{1,0:T(8,128)(2,1)}, u32[]{:S(2)}) copy-start(bf16[192,512]{1,0:T(8,128)(2,1)} %reshape_squeeze.62) | copy-start | bytes 589828
  76.5 4.7 %copy-start.8 = (bf16[192,512]{1,0:T(8,128)(2,1)S(1)}, bf16[192,512]{1,0:T(8,128)(2,1)}, u32[]{:S(2)}) copy-start(bf16[192,512]{1,0:T(8,128)(2,1)} %reshape_squeeze.61) | copy-start | bytes 589828
  76.5 4.7 %copy-start.9 = (bf16[192,512]{1,0:T(8,128)(2,1)S(1)}, bf16[192,512]{1,0:T(8,128)(2,1)}, u32[]{:S(2)}) copy-start(bf16[192,512]{1,0:T(8,128)(2,1)} %reshape_squeeze.58) | copy-start | bytes 589828
  84.6 5.4 %copy-start.17 = (s32[128,8]{0,1:T(8,128)S(1)}, s32[128,8]{0,1:T(8,128)}, u32[]{:S(2)}) copy-start(s32[128,8]{0,1:T(8,128)} %param.19) | copy-start | bytes 12292
  84.6 5.4 %copy-start.18 = (s32[128,8]{0,1:T(8,128)S(1)}, s32[128,8]{0,1:T(8,128)}, u32[]{:S(2)}) copy-start(s32[128,8]{0,1:T(8,128)} %param.18) | copy-start | bytes 12292
  84.6 20.1 %copy-start.16 = (s32[48]{0:T(128)S(1)}, s32[48]{0:T(128)}, u32[]{:S(2)}) copy-start(s32[48]{0:T(128)} %param.20) | copy-start | bytes 580
  84.6 74.0 %all-to-all-start.2 = ((bf16[4,1536,512]{2,1,0:T(8,128)(2,1)}), bf16[4,1536,512]{2,1,0:T(8,128)(2,1)}, u32[]{:S(2)}, u32[]{:S(2)}) async-start(bf16[4,1536,512]{2,1,0:T(8,128)(2,1)} %pad_maximum_fusion.1), calls=%async_computation.2 | async-start | bytes 12582912 | tf_op jit(solution)/shard_map/all_to_all | solution.py:125
  106.6 2.7 copy-start.19
  118.8 45.2 %copy-start.11 = (bf16[128,1536]{1,0:T(8,128)(2,1)S(1)}, bf16[128,1536]{1,0:T(8,128)(2,1)}, u32[]{:S(2)}) copy-start(bf16[128,1536]{1,0:T(8,128)(2,1)} %get-tuple-element.34) | copy-start | bytes 1179652
  158.6 99.2 %all-to-all-start.1 = ((bf16[4,2,8,32,1536]{4,3,2,1,0:T(8,128)(2,1)}), bf16[4,2,8,32,1536]{4,3,2,1,0:T(8,128)(2,1)}, u32[]{:S(2)}, u32[]{:S(2)}) async-start(bf16[4,2,8,32,1536]{4,3,2,1,0:T(8,128)(2,1)} %pad_maximum_fusion), calls=%async_computation.1 | async-start | bytes 12582912 | tf_op jit(solution)/shard_map/all_to_all | solution.py:209
  164.1 77.5 %collective-permute-start = (bf16[128,1536]{1,0:T(8,128)(2,1)S(1)}, bf16[128,1536]{1,0:T(8,128)(2,1)S(1)}, u32[]{:S(2)}, u32[]{:S(2)}) collective-permute-start(bf16[128,1536]{1,0:T(8,128)(2,1)S(1)} %copy-done.11), channel_id=1, source_target_pairs={{8,0},{0,8},{24,16},{16,24},{9,1},{1,9},{25,17},{17,25},{10,2},{2,... | collective-permute-start | bytes 1179656 | tf_op jit(solution)/shard_map/ppermute | solution.py:160
  257.8 3.7 copy-start.2
  261.5 3.4 copy-start.3
  266.8 1.8 copy-start.10
  272.8 5.7 %copy-start.13 = (bf16[1536,40]{0,1:T(8,128)(2,1)S(1)}, bf16[1536,40]{0,1:T(8,128)(2,1)}, u32[]{:S(2)}) copy-start(bf16[1536,40]{0,1:T(8,128)(2,1)} %param.17) | copy-start | bytes 368644
  272.8 74.0 %all-to-all-start.3 = ((bf16[4,2,8,32,1536]{4,3,2,1,0:T(8,128)(2,1)}), bf16[4,2,8,32,1536]{4,3,2,1,0:T(8,128)(2,1)}, u32[]{:S(2)}, u32[]{:S(2)}) async-start(bf16[4,2,8,32,1536]{4,3,2,1,0:T(8,128)(2,1)} %pad_maximum_fusion.2), calls=%async_computation.3 | async-start | bytes 12582912 | tf_op jit(solution)/shard_map/all_to_all | solution.py:250
  278.2 121.6 %reduce-scatter.2.cloned.1.call-start = ((), (), s32[]{:S(2)}) async-start(), calls=%async_computation.6 | async-start | bytes 3538944 | tf_op jit(solution)/shard_map/reduce_scatter | solution.py:266
  356.3 45.7 %copy-start.1 = (bf16[384,1536]{1,0:T(8,128)(2,1)S(1)}, bf16[384,1536]{1,0:T(8,128)(2,1)}, u32[]{:S(2)}) copy-start(bf16[384,1536]{1,0:T(8,128)(2,1)} %param.13) | copy-start | bytes 3538948
  359.0 42.0 %copy-start.15 = (f32[1536]{0:T(1024)S(1)}, f32[1536]{0:T(1024)}, u32[]{:S(2)}) copy-start(f32[1536]{0:T(1024)} %param.16) | copy-start | bytes 18436
  (2 other events, 2.2 us)
Sparse Core Ops, SparseCore 0:
  55.6 37.9 all-gather.1
  359.2 40.5 reduce-scatter.1
